TPU v7x, 256 devices: a whole 4x4x8 slice. The times are simulated.
256 devices in a mesh: dp: 8 (over z), expert: 32 (over y, x, core).
Axes of the slice: x: 4, y: 4, z: 8, core: 2. Of those that a mesh axis runs over, the one named last changes fastest.
Arguments:
- tokens: bfloat16 [32, 16, 7168], P('expert', 'dp'), may hold values from -6 to 6
- tangent: bfloat16 [32, 16, 7168], P('expert', 'dp'), may hold values from -52 to 52
- route_ids: int32 [32, 16, 8], P('expert', 'dp'), may hold values from 0 to 31, all different within a row; in each aligned block of 16 rows (0 to 15, 16 to 31, ..., all dimensions but the last counted through in order) at most 8 rows name the same one
- gate_fixed: int32 [32, 16, 8], P('expert', 'dp'), may hold values from 4096 to 65535
- gate_proj: bfloat16 [32, 7168, 2048], P('expert', None, 'dp'), may hold values from -0.0625 to 0.0625
- up_proj: bfloat16 [32, 7168, 2048], P('expert', None, 'dp'), may hold values from -0.0625 to 0.0625
- down_proj: bfloat16 [32, 2048, 7168], P('expert', 'dp'), may hold values from -0.125 to 0.125
Outputs:
- next_tangent: bfloat16 [32, 16, 7168], P('expert', 'dp')
- lipschitz: float32 [], replicated
Inputs may be any that keep to these rules, and one draw needn't show every extreme that they name: `route_ids`: each token names 8 different experts; within one group of 16 tokens no expert is named by more than 8 tokens.
All inputs are finite; a program needn't handle non-finite values.
Results may differ from a plain program's by a relative error of at most 0.0065.
Values may be sent and summed in bfloat16 or wider, within the bound.
No kernel may reach another device: no remote copies, remote signals or barrier semaphores. Data moves between devices by JAX's collectives and lax.ppermute only.
A program may use at most 128 MiB of HBM per device.

v0:
```python
import jax
import jax.numpy as jnp
from jax import lax
from jax.sharding import PartitionSpec as P


def silu_parts(gate_pre):
    sigmoid_val = jax.nn.sigmoid(gate_pre)
    return (gate_pre * sigmoid_val, sigmoid_val * (1.0 + gate_pre * (1.0 - sigmoid_val)))


def contract_last(left, right):
    return lax.dot_general(
        left, right, (((1,), (1,)), ((), ())), preferred_element_type=jnp.float32
    )


def send_back(partial_value):
    return lax.all_to_all(partial_value, "expert", split_axis=0, concat_axis=0, tiled=True)


def body(tokens, tangent, route_ids, gate_fixed, gate_proj, up_proj, down_proj):
    model_width = tokens.shape[2]
    tok_dev = tokens.shape[1]
    experts = lax.axis_size("expert")
    col_tokens, col_tangent, col_ids, col_gates = (
        lax.all_gather(tokens[0], "dp", axis=0, tiled=True),
        lax.all_gather(tangent[0], "dp", axis=0, tiled=True),
        lax.all_gather(route_ids[0], "dp", axis=0, tiled=True),
        lax.all_gather(gate_fixed[0], "dp", axis=0, tiled=True),
    )
    col_count = col_tokens.shape[0]
    top_count = col_ids.shape[1]
    capacity = min(col_count, 2 * col_count * top_count // experts)
    slot_total = experts * capacity
    flat_ids = col_ids.reshape(-1)
    experts_all = jnp.arange(experts, dtype=jnp.int32)
    onehot = (flat_ids[:, None] == experts_all[None, :]).astype(jnp.int32)
    earlier = jnp.cumsum(onehot, axis=0) - onehot
    slot_place = jnp.sum(earlier * onehot, axis=1)
    target = flat_ids * capacity + slot_place
    places = jnp.arange(slot_total, dtype=jnp.int32)
    matches = target[:, None] == places[None, :]
    route_map = (
        jnp.sum(matches.reshape(col_count, top_count, slot_total), axis=1).astype(jnp.bfloat16).T
    )
    gate_vals = col_gates.reshape(-1).astype(jnp.float32) / 65536.0
    combine_map = jnp.sum(
        jnp.where(matches, gate_vals[:, None], 0.0).reshape(col_count, top_count, slot_total),
        axis=1,
    )
    send_in = (
        jnp.dot(route_map, col_tokens, preferred_element_type=jnp.float32)
        .astype(jnp.bfloat16)
        .reshape(experts, capacity, model_width)
    )
    send_dir = (
        jnp.dot(route_map, col_tangent, preferred_element_type=jnp.float32)
        .astype(jnp.bfloat16)
        .reshape(experts, capacity, model_width)
    )
    weight_gate = gate_proj[0]
    weight_up = up_proj[0]
    weight_down = down_proj[0]
    hidden_dev = weight_gate.shape[1]
    rows_in = lax.all_to_all(send_in, "expert", split_axis=0, concat_axis=0, tiled=True)
    rows_dir = lax.all_to_all(send_dir, "expert", split_axis=0, concat_axis=0, tiled=True)
    groups_here = rows_in.shape[0]
    slots_here = rows_in.shape[1]
    flat_in = rows_in.reshape(-1, model_width)
    flat_dir = rows_dir.reshape(-1, model_width)
    gate_pre = jnp.dot(flat_in, weight_gate, preferred_element_type=jnp.float32)
    up_pre = jnp.dot(flat_in, weight_up, preferred_element_type=jnp.float32)
    gate_dir = jnp.dot(flat_dir, weight_gate, preferred_element_type=jnp.float32)
    up_dir = jnp.dot(flat_dir, weight_up, preferred_element_type=jnp.float32)
    silu_value, silu_slope = silu_parts(gate_pre)
    jvp_hidden = (silu_slope * gate_dir * up_pre + silu_value * up_dir).astype(jnp.bfloat16)
    partial_value = jnp.dot(jvp_hidden, weight_down, preferred_element_type=jnp.float32)
    returned = send_back(partial_value.reshape(groups_here, slots_here, model_width))
    gate_coef = (silu_slope * up_pre).reshape(groups_here, slots_here, hidden_dev)
    up_coef = silu_value.reshape(groups_here, slots_here, hidden_dev)
    returned, gate_coef, up_coef = (returned, gate_coef, up_coef)
    product_part = jnp.dot(
        combine_map,
        returned.reshape(slot_total, -1),
        precision=lax.Precision.HIGHEST,
        preferred_element_type=jnp.float32,
    )
    product_bf = lax.psum(product_part, "dp").astype(jnp.bfloat16)
    send_prod = (
        jnp.dot(route_map, product_bf, preferred_element_type=jnp.float32)
        .astype(jnp.bfloat16)
        .reshape(experts, capacity, model_width)
    )
    received = lax.all_to_all(send_prod, "expert", split_axis=0, concat_axis=0, tiled=True)
    grad_hidden = contract_last(received.reshape(slot_total, model_width), weight_down)
    grad_gate = (grad_hidden * gate_coef.reshape(slot_total, hidden_dev)).astype(jnp.bfloat16)
    grad_up = (grad_hidden * up_coef.reshape(slot_total, hidden_dev)).astype(jnp.bfloat16)
    vjp_part = contract_last(grad_gate, weight_gate) + contract_last(grad_up, weight_up)
    returned_two = send_back(vjp_part.reshape(experts, capacity, model_width))
    result_part = jnp.dot(
        combine_map,
        returned_two.reshape(slot_total, -1),
        precision=lax.Precision.HIGHEST,
        preferred_element_type=jnp.float32,
    )
    result = lax.psum_scatter(result_part, "dp", scatter_dimension=0, tiled=True)
    probe_f = tangent[0].astype(jnp.float32)
    probe_result, result_sq, probe_sq = lax.psum(
        (jnp.sum(probe_f * result), jnp.sum(result * result), jnp.sum(probe_f * probe_f)),
        ("dp", "expert"),
    )
    total_cells = lax.axis_size("dp") * lax.axis_size("expert") * tok_dev * model_width
    next_tangent = (result * lax.rsqrt(result_sq / total_cells + 1e-06)).astype(jnp.bfloat16)
    lipschitz = jnp.sqrt(probe_result / probe_sq)
    return (next_tangent[None], lipschitz)


def solution(mesh):
    return jax.shard_map(
        body,
        mesh=mesh,
        in_specs=(
            P("expert", "dp", None),
            P("expert", "dp", None),
            P("expert", "dp", None),
            P("expert", "dp", None),
            P("expert", None, "dp"),
            P("expert", None, "dp"),
            P("expert", "dp", None),
        ),
        out_specs=(P("expert", "dp", None), P()),
        check_vma=False,
    )
```

profile of v0, /device:TPU:1, one launch (start us, length us, event | category | flops | bytes accessed | tf_op | source)
XLA Modules:
  0.0 622.9 jit_solution(1392663835908994589)
XLA Ops:
  7.2 16.7 %all-gather = s32[1,16,8]{2,0,1:T(1,128)S(1)} all-gather(s32[1,2,8]{2,0,1:T(1,128)} %bitcast.102), channel_id=2, replica_groups=mesh['dp'=8,'expert'=32] {'dp'}, dimensions={1}, use_global_device_ids=true | all-gather | bytes 576 | tf_op jit(solution)/shard_map/all_gather | solution.py:29
  26.8 19.3 %all-gather.2 = bf16[1,16,7168]{2,0,1:T(2,128)(2,1)S(1)} all-gather(bf16[1,2,7168]{2,0,1:T(2,128)(2,1)S(1)} %copy.46), channel_id=4, replica_groups=mesh['dp'=8,'expert'=32] {'dp'}, dimensions={1}, use_global_device_ids=true | all-gather | bytes 258048 | tf_op jit(solution)/shard_map/all_gather | solution.py:27
  46.1 3.0 fusion.1
  49.1 17.6 %all-to-all-start = ((bf16[32,8,7168]{2,1,0:T(8,128)(2,1)}), bf16[32,8,7168]{2,1,0:T(8,128)(2,1)}, u32[]{:S(2)}, u32[]{:S(2)}) async-start(bf16[32,8,7168]{2,1,0:T(8,128)(2,1)} %fusion.1), calls=%async_computation | async-start | bytes 7340032 | tf_op jit(solution)/shard_map/all_to_all | solution.py:66
  66.9 21.6 %all-gather.3 = bf16[1,16,7168]{2,0,1:T(2,128)(2,1)S(1)} all-gather(bf16[1,2,7168]{2,0,1:T(2,128)(2,1)S(1)} %copy.47), channel_id=5, replica_groups=mesh['dp'=8,'expert'=32] {'dp'}, dimensions={1}, use_global_device_ids=true | all-gather | bytes 258048 | tf_op jit(solution)/shard_map/all_gather | solution.py:28
  88.4 3.0 fusion.2
  91.4 20.8 %all-to-all-done = bf16[32,8,7168]{2,1,0:T(8,128)(2,1)} async-done(((bf16[32,8,7168]{2,1,0:T(8,128)(2,1)}), bf16[32,8,7168]{2,1,0:T(8,128)(2,1)}, u32[]{:S(2)}, u32[]{:S(2)}) %all-to-all-start) | async-done | bytes 3670048 | tf_op jit(solution)/shard_map/all_to_all | solution.py:66
  112.2 7.2 %all-to-all-start.1 = ((bf16[32,8,7168]{2,1,0:T(8,128)(2,1)}), bf16[32,8,7168]{2,1,0:T(8,128)(2,1)}, u32[]{:S(2)}, u32[]{:S(2)}) async-start(bf16[32,8,7168]{2,1,0:T(8,128)(2,1)} %fusion.2), calls=%async_computation.1 | async-start | bytes 7340032 | tf_op jit(solution)/shard_map/all_to_all | solution.py:67
  119.5 4.4 fusion.24
  123.9 3.2 fusion.16
  127.1 37.5 %all-to-all-done.1 = bf16[32,8,7168]{2,1,0:T(8,128)(2,1)} async-done(((bf16[32,8,7168]{2,1,0:T(8,128)(2,1)}), bf16[32,8,7168]{2,1,0:T(8,128)(2,1)}, u32[]{:S(2)}, u32[]{:S(2)}) %all-to-all-start.1) | async-done | bytes 3670048 | tf_op jit(solution)/shard_map/all_to_all | solution.py:67
  164.6 4.3 fusion.43
  168.9 11.2 %fusion.10 = f32[32,8,7168]{2,1,0:T(8,128)} fusion(bf16[1,256,7168]{2,1,0:T(8,128)(2,1)} %param.13, f32[256,256]{1,0:T(8,128)S(1)} %fusion.43, f32[256,256]{1,0:T(8,128)S(1)} %fusion.16, bf16[1,7168,256]{2,1,0:T(8,128)(2,1)} %param.11, bf16[32,8,7168]{2,1,0:T(8,128)(2,1)} %all-to-all-done.1, f32[256,256]{1,0:T(8,128)S(1)} %fusion.24), kind=kOutput, calls=%fused_computation.14 | convolution fusion | flops 1879769088 | bytes 19136512 | tf_op jit(solution)/shard_map/dot_general | solution.py:78
  180.0 7.8 %all-to-all-start.2 = ((f32[32,8,7168]{2,1,0:T(8,128)}), f32[32,8,7168]{2,1,0:T(8,128)}, u32[]{:S(2)}, u32[]{:S(2)}) async-start(f32[32,8,7168]{2,1,0:T(8,128)} %fusion.10), calls=%async_computation.2 | async-start | bytes 14680064 | tf_op jit(solution)/shard_map/all_to_all | solution.py:19
  187.9 11.6 %all-gather.1 = s32[1,16,8]{2,0,1:T(1,128)S(1)} all-gather(s32[1,2,8]{2,0,1:T(1,128)S(1)} %bitcast.103), channel_id=3, replica_groups=mesh['dp'=8,'expert'=32] {'dp'}, dimensions={1}, use_global_device_ids=true | all-gather | bytes 576 | tf_op jit(solution)/shard_map/all_gather | solution.py:30
  199.8 75.2 %all-to-all-done.2 = f32[32,8,7168]{2,1,0:T(8,128)} async-done(((f32[32,8,7168]{2,1,0:T(8,128)}), f32[32,8,7168]{2,1,0:T(8,128)}, u32[]{:S(2)}, u32[]{:S(2)}) %all-to-all-start.2) | async-done | bytes 7340064 | tf_op jit(solution)/shard_map/all_to_all | solution.py:19
  275.0 5.7 fusion.6
  280.7 26.0 %all-reduce.6 = bf16[16,7168]{1,0:T(8,128)(2,1)S(1)} all-reduce(f32[16,7168]{1,0:T(8,128)S(1)} %fusion.6), channel_id=1, replica_groups=mesh['dp'=8,'expert'=32] {'dp'}, use_global_device_ids=true, to_apply=%region_4.5 | all-reduce | flops 114688 | bytes 688128 | tf_op jit(solution)/shard_map/psum | solution.py:89
  307.8 60.0 %all_to_all.25 = bf16[32,8,7168]{2,1,0:T(8,128)(2,1)S(1)} all-to-all(bf16[32,8,7168]{2,1,0:T(8,128)(2,1)S(1)} %fusion.3), channel_id=1, replica_groups=mesh['dp'=8,'expert'=32] {'expert'}, dimensions={0} | all-to-all | bytes 7340032 | tf_op jit(solution)/shard_map/all_to_all | solution.py:95
  373.1 88.2 %all_to_all.26 = f32[32,8,7168]{2,1,0:T(8,128)S(1)} all-to-all(f32[32,8,7168]{2,1,0:T(8,128)S(1)} %fusion), channel_id=1, replica_groups=mesh['dp'=8,'expert'=32] {'expert'}, dimensions={0} | all-to-all | bytes 14680064 | tf_op jit(solution)/shard_map/all_to_all | solution.py:19
  461.4 4.3 fusion.4
  467.0 62.5 %all-reduce.5.cloned.1.call-done = f32[16,7168]{1,0:T(8,128)} async-done(((f32[16,7168]{1,0:T(8,128)}), f32[16,7168]{1,0:T(8,128)}) %all-reduce.5.cloned.1.call-update) | async-done | bytes 458768
  529.5 1.7 fusion.69
  531.2 80.1 %all-reduce.1 = (f32[]{:T(128)}, f32[]{:T(128)}, f32[]{:T(128)}) all-reduce(f32[]{:T(128)} %get-tuple-element.3, f32[]{:T(128)} %get-tuple-element.2, f32[]{:T(128)} %get-tuple-element.4), channel_id=1, replica_groups=mesh['dp'=8,'expert'=32] {'dp','expert'}, use_global_device_ids=true, to_apply=%region_7.8 | all-reduce | flops 3 | bytes 24 | tf_op jit(solution)/shard_map/psum | solution.py:109
  (40 shorter events, 11.9 us)
Async XLA Ops:
  49.1 17.7 %copy-start.4 = (bf16[1,2,7168]{2,1,0:T(2,128)(2,1)S(1)}, bf16[1,2,7168]{2,1,0:T(2,128)(2,1)}, u32[]{:S(2)}) copy-start(bf16[1,2,7168]{2,1,0:T(2,128)(2,1)} %param.8) | copy-start | bytes 86020
  49.1 63.1 %all-to-all-start = ((bf16[32,8,7168]{2,1,0:T(8,128)(2,1)}), bf16[32,8,7168]{2,1,0:T(8,128)(2,1)}, u32[]{:S(2)}, u32[]{:S(2)}) async-start(bf16[32,8,7168]{2,1,0:T(8,128)(2,1)} %fusion.1), calls=%async_computation | async-start | bytes 7340032 | tf_op jit(solution)/shard_map/all_to_all | solution.py:66
  112.2 52.4 %all-to-all-start.1 = ((bf16[32,8,7168]{2,1,0:T(8,128)(2,1)}), bf16[32,8,7168]{2,1,0:T(8,128)(2,1)}, u32[]{:S(2)}, u32[]{:S(2)}) async-start(bf16[32,8,7168]{2,1,0:T(8,128)(2,1)} %fusion.2), calls=%async_computation.1 | async-start | bytes 7340032 | tf_op jit(solution)/shard_map/all_to_all | solution.py:67
  119.4 4.4 copy-start.2
  180.0 7.9 %copy-start.5 = (s32[1,2,8]{2,1,0:T(2,128)S(1)}, s32[1,2,8]{2,1,0:T(2,128)}, u32[]{:S(2)}) copy-start(s32[1,2,8]{2,1,0:T(2,128)} %param.10) | copy-start | bytes 196
  180.0 95.0 %all-to-all-start.2 = ((f32[32,8,7168]{2,1,0:T(8,128)}), f32[32,8,7168]{2,1,0:T(8,128)}, u32[]{:S(2)}, u32[]{:S(2)}) async-start(f32[32,8,7168]{2,1,0:T(8,128)} %fusion.10), calls=%async_computation.2 | async-start | bytes 14680064 | tf_op jit(solution)/shard_map/all_to_all | solution.py:19
  187.8 341.6 %all-reduce.5.cloned.1.call-start = ((), (), s32[]{:S(2)}) async-start(), calls=%async_computation.5 | async-start | bytes 917504
  307.8 60.0 %copy-start.1 = (bf16[1,256,7168]{2,1,0:T(8,128)(2,1)S(1)}, bf16[1,256,7168]{2,1,0:T(8,128)(2,1)}, u32[]{:S(2)}) copy-start(bf16[1,256,7168]{2,1,0:T(8,128)(2,1)} %param.13) | copy-start | bytes 11010052
  367.9 2.0 copy-start
  369.9 2.0 copy-start.3
  461.4 4.4 copy-start.6
Sparse Core Ops, SparseCore 0:
  465.8 63.5 all-reduce.4
where the time goes:
time: 624 us; the launch traced here: 623 us
  blocking collectives  323 us (52%)
  waiting for transfers between devices  196 us (31%)
  matrix products  43.7 us (7%)
  starting transfers between devices  32.7 us (5%)
  between operations  18.1 us (3%)
    all_to_all x1, blocking collectives, send_back(): lax.all_to_all(partial_value, 'expert', split_axis=0, concat_axis=0, tile...  88.2 us
    psum x1, blocking collectives, body(): lax.psum((jnp.sum(probe_f * result), jnp.sum(result * result), jnp.sum(pr...  80.1 us
    all_to_all x1, waiting for transfers between devices, send_back(): lax.all_to_all(partial_value, 'expert', split_axis=0, concat_axis=0, tile...  75.2 us
    unnamed x2, waiting for transfers between devices  62.5 us
    all_to_all x1, blocking collectives, body(): lax.all_to_all(send_prod, 'expert', split_axis=0, concat_axis=0, tiled=True)  60 us
    all_to_all x1, waiting for transfers between devices, body(): lax.all_to_all(send_dir, 'expert', split_axis=0, concat_axis=0, tiled=True)  37.5 us
    psum x1, blocking collectives, body(): product_bf = lax.psum(product_part, 'dp').astype(jnp.bfloat16)  26 us
    all_gather x1, blocking collectives, body(): lax.all_gather(tangent[0], 'dp', axis=0, tiled=True)  21.6 us
  transfers between devices with their start and end apart: 4, of which 4 were waited for; matrix products, arithmetic and copies ran while one was open for 2% of the time, Pallas kernels for 0%

commit v1 on v0

v1 whole, which is shorter than its diff:
```python
import jax
import jax.numpy as jnp
from jax import lax
from jax.sharding import PartitionSpec as P

BF16 = jnp.bfloat16
F32 = jnp.float32


def silu_parts(gate_pre):
    sigmoid_val = jax.nn.sigmoid(gate_pre)
    return (gate_pre * sigmoid_val, sigmoid_val * (1.0 + gate_pre * (1.0 - sigmoid_val)))


def contract_last(left, right):
    return lax.dot_general(
        left, right, (((1,), (1,)), ((), ())), preferred_element_type=F32
    )


def exchange(value):
    return lax.all_to_all(value, "expert", split_axis=0, concat_axis=0, tiled=True)


def body(tokens, tangent, route_ids, gate_fixed, gate_proj, up_proj, down_proj):
    model_width = tokens.shape[2]
    tok_dev = tokens.shape[1]
    top_count = route_ids.shape[2]
    experts = lax.axis_size("expert")
    gates_local = gate_fixed[0]
    pieces = [
        tokens[0],
        tangent[0],
        route_ids[0].astype(BF16),
        (gates_local // 256).astype(BF16),
        (gates_local % 256).astype(BF16),
    ]
    width = 2 * model_width + 3 * top_count
    pad = (-width) % 128
    if pad:
        pieces.append(jnp.zeros((tok_dev, pad), BF16))
    packed = jnp.concatenate(pieces, axis=1)
    col = lax.all_gather(packed, "dp", axis=0, tiled=True)
    col_count = col.shape[0]
    meta = col[:, 2 * model_width: width].astype(jnp.int32)
    col_ids = meta[:, :top_count]
    col_gates = meta[:, top_count: 2 * top_count] * 256 + meta[:, 2 * top_count:]
    col_pair = jnp.concatenate(
        [col[:, :model_width], col[:, model_width: 2 * model_width]], axis=0
    )

    capacity = min(col_count, 2 * col_count * top_count // experts)
    slot_total = experts * capacity
    flat_ids = col_ids.reshape(-1)
    experts_all = jnp.arange(experts, dtype=jnp.int32)
    onehot = (flat_ids[:, None] == experts_all[None, :]).astype(jnp.int32)
    earlier = jnp.cumsum(onehot, axis=0) - onehot
    slot_place = jnp.sum(earlier * onehot, axis=1)
    target = flat_ids * capacity + slot_place
    places = jnp.arange(slot_total, dtype=jnp.int32)
    matches = target[:, None] == places[None, :]
    route_f = jnp.sum(
        matches.reshape(col_count, top_count, slot_total), axis=1
    ).astype(F32).T
    route_map = route_f.astype(BF16)
    gate_vals = col_gates.reshape(-1).astype(F32) / 65536.0
    combine_map = jnp.sum(
        jnp.where(matches, gate_vals[:, None], 0.0).reshape(col_count, top_count, slot_total),
        axis=1,
    )
    eye2 = jnp.eye(2, dtype=F32)
    pair_map = (
        route_f.reshape(experts, 1, capacity, 1, col_count)
        * eye2.reshape(1, 2, 1, 2, 1)
    ).reshape(experts * 2 * capacity, 2 * col_count).astype(BF16)
    send_pair = (
        jnp.dot(pair_map, col_pair, preferred_element_type=F32)
        .astype(BF16)
        .reshape(experts, 2 * capacity, model_width)
    )
    weight_gate = gate_proj[0]
    weight_up = up_proj[0]
    weight_down = down_proj[0]
    hidden_dev = weight_gate.shape[1]
    rows_pair = exchange(send_pair)
    groups_here = rows_pair.shape[0]
    flat_pair = rows_pair.reshape(-1, model_width)
    gate_both = jnp.dot(flat_pair, weight_gate, preferred_element_type=F32).reshape(
        groups_here, 2, capacity, hidden_dev
    )
    up_both = jnp.dot(flat_pair, weight_up, preferred_element_type=F32).reshape(
        groups_here, 2, capacity, hidden_dev
    )
    gate_pre = gate_both[:, 0].reshape(-1, hidden_dev)
    gate_dir = gate_both[:, 1].reshape(-1, hidden_dev)
    up_pre = up_both[:, 0].reshape(-1, hidden_dev)
    up_dir = up_both[:, 1].reshape(-1, hidden_dev)
    silu_value, silu_slope = silu_parts(gate_pre)
    jvp_hidden = (silu_slope * gate_dir * up_pre + silu_value * up_dir).astype(BF16)
    partial_value = jnp.dot(jvp_hidden, weight_down, preferred_element_type=F32)
    returned = exchange(
        partial_value.astype(BF16).reshape(groups_here, capacity, model_width)
    )
    gate_coef = silu_slope * up_pre
    up_coef = silu_value
    product_part = jnp.dot(
        combine_map,
        returned.reshape(slot_total, -1).astype(F32),
        precision=lax.Precision.HIGHEST,
        preferred_element_type=F32,
    )
    product_bf = lax.psum(product_part, "dp").astype(BF16)
    send_prod = (
        jnp.dot(route_map, product_bf, preferred_element_type=F32)
        .astype(BF16)
        .reshape(experts, capacity, model_width)
    )
    received = exchange(send_prod)
    grad_hidden = contract_last(received.reshape(slot_total, model_width), weight_down)
    grad_gate = (grad_hidden * gate_coef).astype(BF16)
    grad_up = (grad_hidden * up_coef).astype(BF16)
    vjp_part = contract_last(grad_gate, weight_gate) + contract_last(grad_up, weight_up)
    returned_two = exchange(
        vjp_part.astype(BF16).reshape(experts, capacity, model_width)
    )
    result_part = jnp.dot(
        combine_map,
        returned_two.reshape(slot_total, -1).astype(F32),
        precision=lax.Precision.HIGHEST,
        preferred_element_type=F32,
    )
    result = lax.psum_scatter(result_part, "dp", scatter_dimension=0, tiled=True)
    probe_f = tangent[0].astype(F32)
    probe_result, result_sq, probe_sq = lax.psum(
        (jnp.sum(probe_f * result), jnp.sum(result * result), jnp.sum(probe_f * probe_f)),
        ("dp", "expert"),
    )
    total_cells = lax.axis_size("dp") * lax.axis_size("expert") * tok_dev * model_width
    next_tangent = (result * lax.rsqrt(result_sq / total_cells + 1e-06)).astype(BF16)
    lipschitz = jnp.sqrt(probe_result / probe_sq)
    return (next_tangent[None], lipschitz)


def solution(mesh):
    return jax.shard_map(
        body,
        mesh=mesh,
        in_specs=(
            P("expert", "dp", None),
            P("expert", "dp", None),
            P("expert", "dp", None),
            P("expert", "dp", None),
            P("expert", None, "dp"),
            P("expert", None, "dp"),
            P("expert", "dp", None),
        ),
        out_specs=(P("expert", "dp", None), P()),
        check_vma=False,
    )
```

time: 624 us -> 497 us (0.80)
  waiting for transfers between devices: 196 us -> 107 us
  starting transfers between devices: 32.7 us -> 4.86 us
  matrix products: 43.7 us -> 19.7 us
  blocking collectives: 323 us -> 337 us
    all_to_all x3 -> x1, waiting for transfers between devices: 134 us -> 44.9 us  [exchange(): lax.all_to_all(value, 'expert', split_axis=0, concat_axis=0, tiled=True)]
    all_to_all x2 -> x3, blocking collectives: 148 us -> 205 us  [exchange(): lax.all_to_all(value, 'expert', split_axis=0, concat_axis=0, tiled=True)]
    all_gather x4 -> x1, blocking collectives: 69.2 us -> 23.7 us  [body(): col = lax.all_gather(packed, 'dp', axis=0, tiled=True)]
    all_to_all x3 -> x1, starting transfers between devices: 32.7 us -> 4.82 us  [exchange(): lax.all_to_all(value, 'expert', split_axis=0, concat_axis=0, tiled=True)]
    dot_general x9 -> x7, matrix products: 40.2 us -> 16.2 us  [the longest x1 3.57 us: body(): jnp.dot(combine_map, returned.reshape(slot_total, -1).astype(F32), precis...]
  transfers between devices with their start and end apart: 4 -> 2, of which waited for: 4 -> 2; matrix products, arithmetic and copies ran while one was open for 2% -> 0% of each run, Pallas kernels for 0% -> 0%
where the time goes in v1:
time: 497 us; the launch traced here: 496 us
  blocking collectives  337 us (68%)
  waiting for transfers between devices  107 us (22%)
  matrix products  19.7 us (4%)
  between operations  18.1 us (4%)
  other arithmetic  5.68 us (1%)
    all_to_all x3, blocking collectives, exchange(): lax.all_to_all(value, 'expert', split_axis=0, concat_axis=0, tiled=True)  205 us
    psum x1, blocking collectives, body(): lax.psum((jnp.sum(probe_f * result), jnp.sum(result * result), jnp.sum(pr...  80.1 us
    unnamed x2, waiting for transfers between devices  62.1 us
    all_to_all x1, waiting for transfers between devices, exchange(): lax.all_to_all(value, 'expert', split_axis=0, concat_axis=0, tiled=True)  44.9 us
    psum x1, blocking collectives, body(): product_bf = lax.psum(product_part, 'dp').astype(BF16)  28.2 us
    all_gather x1, blocking collectives, body(): col = lax.all_gather(packed, 'dp', axis=0, tiled=True)  23.7 us
  transfers between devices with their start and end apart: 2, of which 2 were waited for; matrix products, arithmetic and copies ran while one was open for 0% of the time, Pallas kernels for 0%

profile of v1, /device:TPU:1, one launch (start us, length us, event | category | flops | bytes accessed | tf_op | source)
XLA Modules:
  0.0 496.2 jit_solution(14524132102642386330)
XLA Ops:
  8.6 0.9 concatenate.6
  9.4 23.7 %all-gather = bf16[8,2,14464]{2,1,0:T(2,128)(2,1)S(1)} all-gather(bf16[1,2,14464]{2,1,0:T(2,128)(2,1)S(1)} %bitcast.125), channel_id=1, replica_groups=mesh['dp'=8,'expert'=32] {'dp'}, dimensions={0}, use_global_device_ids=true | all-gather | bytes 520704 | tf_op jit(solution)/shard_map/all_gather | solution.py:43
  34.6 2.0 convolution_convert_fusion
  36.7 98.5 %all_to_all.20 = bf16[32,16,7168]{2,1,0:T(8,128)(2,1)S(1)} all-to-all(bf16[32,16,7168]{2,1,0:T(8,128)(2,1)S(1)} %bitcast.123), channel_id=1, replica_groups=mesh['dp'=8,'expert'=32] {'expert'}, dimensions={0} | all-to-all | bytes 14680064 | tf_op jit(solution)/shard_map/all_to_all | solution.py:22
  135.2 2.1 fusion.6
  137.2 2.1 fusion.4
  139.3 3.1 fusion.1
  142.4 4.8 all-to-all-start.1
  147.4 44.9 %all-to-all-done.1 = bf16[32,8,7168]{2,1,0:T(8,128)(2,1)} async-done(((bf16[32,8,7168]{2,1,0:T(8,128)(2,1)}), bf16[32,8,7168]{2,1,0:T(8,128)(2,1)}, u32[]{:S(2)}, u32[]{:S(2)}) %all-to-all-start.1) | async-done | bytes 3670048 | tf_op jit(solution)/shard_map/all_to_all | solution.py:22
  192.3 3.6 fusion.14
  195.9 28.2 %all-reduce.6 = bf16[16,7168]{1,0:T(8,128)(2,1)S(1)} all-reduce(f32[16,7168]{1,0:T(8,128)S(1)} %fusion.14), channel_id=1, replica_groups=mesh['dp'=8,'expert'=32] {'dp'}, use_global_device_ids=true, to_apply=%region_4.5 | all-reduce | flops 114688 | bytes 688128 | tf_op jit(solution)/shard_map/psum | solution.py:112
  224.1 1.1 fusion.2
  225.3 57.6 %all_to_all.21 = bf16[32,8,7168]{2,1,0:T(8,128)(2,1)S(1)} all-to-all(bf16[32,8,7168]{2,1,0:T(8,128)(2,1)S(1)} %fusion.2), channel_id=1, replica_groups=mesh['dp'=8,'expert'=32] {'expert'}, dimensions={0} | all-to-all | bytes 7340032 | tf_op jit(solution)/shard_map/all_to_all | solution.py:22
  282.9 1.1 fusion.12
  284.0 0.9 copy-done.3
  284.9 1.2 fusion.19
  286.1 0.8 copy-done.5
  287.0 1.2 fusion.3
  288.1 48.9 %all_to_all.22 = bf16[32,8,7168]{2,1,0:T(8,128)(2,1)S(1)} all-to-all(bf16[32,8,7168]{2,1,0:T(8,128)(2,1)S(1)} %fusion.3), channel_id=1, replica_groups=mesh['dp'=8,'expert'=32] {'expert'}, dimensions={0} | all-to-all | bytes 7340032 | tf_op jit(solution)/shard_map/all_to_all | solution.py:22
  337.0 2.3 fusion.10
  340.6 62.1 %all-reduce.5.cloned.1.call-done = f32[16,7168]{1,0:T(8,128)} async-done(((f32[16,7168]{1,0:T(8,128)}), f32[16,7168]{1,0:T(8,128)}) %all-reduce.5.cloned.1.call-update) | async-done | bytes 458768
  402.8 1.7 fusion.44
  404.5 80.1 %all-reduce.1 = (f32[]{:T(128)}, f32[]{:T(128)}, f32[]{:T(128)}) all-reduce(f32[]{:T(128)} %get-tuple-element.3, f32[]{:T(128)} %get-tuple-element.2, f32[]{:T(128)} %get-tuple-element.4), channel_id=1, replica_groups=mesh['dp'=8,'expert'=32] {'dp','expert'}, use_global_device_ids=true, to_apply=%region_7.8 | all-reduce | flops 3 | bytes 24 | tf_op jit(solution)/shard_map/psum | solution.py:134
  486.6 1.6 fusion.46
  (37 shorter events, 3.7 us)
Async XLA Ops:
  36.7 98.5 %copy-start.2 = (bf16[1,7168,256]{2,1,0:T(8,128)(2,1)S(1)}, bf16[1,7168,256]{2,1,0:T(8,128)(2,1)}, u32[]{:S(2)}) copy-start(bf16[1,7168,256]{2,1,0:T(8,128)(2,1)} %param.11) | copy-start | bytes 11010052
  135.2 2.1 copy-start.4
  137.2 2.1 copy-start
  142.4 50.0 %all-to-all-start.1 = ((bf16[32,8,7168]{2,1,0:T(8,128)(2,1)}), bf16[32,8,7168]{2,1,0:T(8,128)(2,1)}, u32[]{:S(2)}, u32[]{:S(2)}) async-start(bf16[32,8,7168]{2,1,0:T(8,128)(2,1)} %fusion.1), calls=%async_computation.1 | async-start | bytes 7340032 | tf_op jit(solution)/shard_map/all_to_all | solution.py:22
  147.2 255.6 %all-reduce.5.cloned.1.call-start = ((), (), s32[]{:S(2)}) async-start(), calls=%async_computation.4 | async-start | bytes 917504
  225.3 57.6 %copy-start.1 = (bf16[1,256,7168]{2,1,0:T(8,128)(2,1)S(1)}, bf16[1,256,7168]{2,1,0:T(8,128)(2,1)}, u32[]{:S(2)}) copy-start(bf16[1,256,7168]{2,1,0:T(8,128)(2,1)} %param.13) | copy-start | bytes 11010052
  282.9 2.0 copy-start.3
  284.9 2.0 copy-start.5
  337.0 2.4 copy-start.7
  337.0 65.7 %copy-start.6 = (bf16[1,2,7168]{2,1,0:T(2,128)(2,1)S(1)}, bf16[1,2,7168]{2,1,0:T(2,128)(2,1)}, u32[]{:S(2)}) copy-start(bf16[1,2,7168]{2,1,0:T(2,128)(2,1)} %param.8) | copy-start | bytes 86020
Sparse Core Ops, SparseCore 0:
  339.5 63.2 all-reduce.4

commit v2 on v1

--- a/solution.py
+++ b/solution.py
@@ -22,6 +22,39 @@
     return lax.all_to_all(value, "expert", split_axis=0, concat_axis=0, tiled=True)
 
 
+def shifted(value, axis, size, step):
+    return lax.ppermute(value, axis, [(i, (i + step) % size) for i in range(size)])
+
+
+def gather_rows(value, axis):
+    size = lax.axis_size(axis)
+    me = lax.axis_index(axis)
+    got = jnp.stack([value] + [shifted(value, axis, size, s) for s in range(1, size)])
+    source_slot = (me - jnp.arange(size)) % size
+    order = jnp.zeros((size,), jnp.int32).at[source_slot].set(jnp.arange(size))
+    return got[order].reshape(size * value.shape[0], *value.shape[1:])
+
+
+def scatter_sum_rows(value, axis):
+    size = lax.axis_size(axis)
+    me = lax.axis_index(axis)
+    blocks = value.reshape(size, value.shape[0] // size, *value.shape[1:])
+    total = lax.dynamic_index_in_dim(blocks, me, 0, keepdims=False)
+    for s in range(1, size):
+        outgoing = lax.dynamic_index_in_dim(blocks, (me + s) % size, 0, keepdims=False)
+        total = total + shifted(outgoing, axis, size, s)
+    return total
+
+
+def butterfly_sum(value, axis):
+    size = lax.axis_size(axis)
+    step = 1
+    while step < size:
+        value = value + lax.ppermute(value, axis, [(i, i ^ step) for i in range(size)])
+        step *= 2
+    return value
+
+
 def body(tokens, tangent, route_ids, gate_fixed, gate_proj, up_proj, down_proj):
     model_width = tokens.shape[2]
     tok_dev = tokens.shape[1]
@@ -40,7 +73,7 @@
     if pad:
         pieces.append(jnp.zeros((tok_dev, pad), BF16))
     packed = jnp.concatenate(pieces, axis=1)
-    col = lax.all_gather(packed, "dp", axis=0, tiled=True)
+    col = gather_rows(packed, "dp")
     col_count = col.shape[0]
     meta = col[:, 2 * model_width: width].astype(jnp.int32)
     col_ids = meta[:, :top_count]
@@ -129,12 +162,13 @@
         precision=lax.Precision.HIGHEST,
         preferred_element_type=F32,
     )
-    result = lax.psum_scatter(result_part, "dp", scatter_dimension=0, tiled=True)
+    result = scatter_sum_rows(result_part, "dp")
     probe_f = tangent[0].astype(F32)
-    probe_result, result_sq, probe_sq = lax.psum(
-        (jnp.sum(probe_f * result), jnp.sum(result * result), jnp.sum(probe_f * probe_f)),
-        ("dp", "expert"),
+    sums = jnp.stack(
+        [jnp.sum(probe_f * result), jnp.sum(result * result), jnp.sum(probe_f * probe_f)]
     )
+    sums = butterfly_sum(butterfly_sum(sums, "dp"), "expert")
+    probe_result, result_sq, probe_sq = sums[0], sums[1], sums[2]
     total_cells = lax.axis_size("dp") * lax.axis_size("expert") * tok_dev * model_width
     next_tangent = (result * lax.rsqrt(result_sq / total_cells + 1e-06)).astype(BF16)
     lipschitz = jnp.sqrt(probe_result / probe_sq)

time: 497 us -> 400 us (0.80)
  blocking collectives: 337 us -> 179 us
  starting transfers between devices: 4.86 us -> 55.8 us
  between operations: 18.1 us -> 4.3 us
  waiting for transfers between devices: 107 us -> 117 us
    psum x1 -> x0, blocking collectives: 80.1 us -> none  [body(): lax.psum((jnp.sum(probe_f * result), jnp.sum(result * result), jnp.sum(pr...]
    unnamed x2 -> x0, waiting for transfers between devices: 62.1 us -> none
    all_to_all x3 -> x2, blocking collectives: 205 us -> 150 us  [exchange(): lax.all_to_all(value, 'expert', split_axis=0, concat_axis=0, tiled=True)]
    ppermute x0 -> x22, starting transfers between devices: none -> 46 us  [the longest x14 28.3 us: shifted(): lax.ppermute(value, axis, [(i, (i + step) % size) for i in range(size)])]
    all_to_all x1 -> x2, waiting for transfers between devices: 44.9 us -> 90 us  [exchange(): lax.all_to_all(value, 'expert', split_axis=0, concat_axis=0, tiled=True)]
    ppermute x0 -> x22, waiting for transfers between devices: none -> 27.2 us  [the longest x8 18.2 us: butterfly_sum(): lax.ppermute(value, axis, [(i, i ^ step) for i in range(size)])]
    all_gather x1 -> x0, blocking collectives: 23.7 us -> none  [body(): col = lax.all_gather(packed, 'dp', axis=0, tiled=True)]
    all_to_all x1 -> x2, starting transfers between devices: 4.82 us -> 9.83 us  [exchange(): lax.all_to_all(value, 'expert', split_axis=0, concat_axis=0, tiled=True)]
  transfers between devices with their start and end apart: 2 -> 24, of which waited for: 2 -> 14; matrix products, arithmetic and copies ran while one was open for 0% -> 0% of each run, Pallas kernels for 0% -> 0%
where the time goes in v2:
time: 400 us; the launch traced here: 396 us
  blocking collectives  179 us (45%)
  waiting for transfers between devices  117 us (29%)
  starting transfers between devices  55.8 us (14%)
  matrix products  22.8 us (6%)
  other arithmetic  9.87 us (2%)
  local copies, waits for them, and re-layouts  6.96 us (2%)
  between operations  4.3 us (1%)
    all_to_all x2, blocking collectives, exchange(): lax.all_to_all(value, 'expert', split_axis=0, concat_axis=0, tiled=True)  150 us
    all_to_all x2, waiting for transfers between devices, exchange(): lax.all_to_all(value, 'expert', split_axis=0, concat_axis=0, tiled=True)  90 us
    ppermute x14, starting transfers between devices, shifted(): lax.ppermute(value, axis, [(i, (i + step) % size) for i in range(size)])  28.3 us
    psum x1, blocking collectives, body(): product_bf = lax.psum(product_part, 'dp').astype(BF16)  28.3 us
    ppermute x8, waiting for transfers between devices, butterfly_sum(): lax.ppermute(value, axis, [(i, i ^ step) for i in range(size)])  18.2 us
    ppermute x8, starting transfers between devices, butterfly_sum(): lax.ppermute(value, axis, [(i, i ^ step) for i in range(size)])  17.7 us
    all_to_all x2, starting transfers between devices, exchange(): lax.all_to_all(value, 'expert', split_axis=0, concat_axis=0, tiled=True)  9.83 us
    ppermute x14, waiting for transfers between devices, shifted(): lax.ppermute(value, axis, [(i, (i + step) % size) for i in range(size)])  8.95 us
  transfers between devices with their start and end apart: 24, of which 14 were waited for; matrix products, arithmetic and copies ran while one was open for 0% of the time, Pallas kernels for 0%

profile of v2, /device:TPU:1, one launch (start us, length us, event | category | flops | bytes accessed | tf_op | source)
XLA Modules:
  0.0 395.6 jit_solution(4089663830827276678)
XLA Ops:
  2.9 2.5 collective-permute-start
  5.4 3.0 collective-permute-start.1
  8.4 3.8 collective-permute-start.2
  12.6 4.5 %collective-permute-start.4 = (bf16[2,14464]{1,0:T(2,128)(2,1)S(1)}, bf16[2,14464]{1,0:T(2,128)(2,1)S(1)}, u32[]{:S(2)}, u32[]{:S(2)}) collective-permute-start(bf16[2,14464]{1,0:T(2,128)(2,1)S(1)} %concatenate.6), channel_id=1, source_target_pairs={{0,160},{32,192},{64,224},{96,0},{128,32},{160,64},{192,96},{224,1... | collective-permute-start | bytes 173576 | tf_op jit(solution)/shard_map/ppermute | solution.py:26
  21.4 5.1 %collective-permute-done.5 = bf16[2,14464]{1,0:T(2,128)(2,1)S(1)} collective-permute-done((bf16[2,14464]{1,0:T(2,128)(2,1)S(1)}, bf16[2,14464]{1,0:T(2,128)(2,1)S(1)}, u32[]{:S(2)}, u32[]{:S(2)}) %collective-permute-start.5) | collective-permute-done | bytes 57888 | tf_op jit(solution)/shard_map/ppermute | solution.py:26
  31.7 93.0 %all_to_all.20 = bf16[32,16,7168]{2,1,0:T(8,128)(2,1)S(1)} all-to-all(bf16[32,16,7168]{2,1,0:T(8,128)(2,1)S(1)} %bitcast.181), channel_id=1, replica_groups=mesh['dp'=8,'expert'=32] {'expert'}, dimensions={0} | all-to-all | bytes 14680064 | tf_op jit(solution)/shard_map/all_to_all | solution.py:22
  128.8 3.1 fusion.1
  131.9 4.8 %all-to-all-start.1 = ((bf16[32,8,7168]{2,1,0:T(8,128)(2,1)}), bf16[32,8,7168]{2,1,0:T(8,128)(2,1)}, u32[]{:S(2)}, u32[]{:S(2)}) async-start(bf16[32,8,7168]{2,1,0:T(8,128)(2,1)} %fusion.1), calls=%async_computation.1 | async-start | bytes 7340032 | tf_op jit(solution)/shard_map/all_to_all | solution.py:22
  136.9 44.9 %all-to-all-done.1 = bf16[32,8,7168]{2,1,0:T(8,128)(2,1)} async-done(((bf16[32,8,7168]{2,1,0:T(8,128)(2,1)}), bf16[32,8,7168]{2,1,0:T(8,128)(2,1)}, u32[]{:S(2)}, u32[]{:S(2)}) %all-to-all-start.1) | async-done | bytes 3670048 | tf_op jit(solution)/shard_map/all_to_all | solution.py:22
  181.9 3.6 fusion.14
  185.5 28.3 %all-reduce.1 = bf16[16,7168]{1,0:T(8,128)(2,1)S(1)} all-reduce(f32[16,7168]{1,0:T(8,128)S(1)} %fusion.14), channel_id=1, replica_groups=mesh['dp'=8,'expert'=32] {'dp'}, use_global_device_ids=true, to_apply=%region_5.6 | all-reduce | flops 114688 | bytes 688128 | tf_op jit(solution)/shard_map/psum | solution.py:145
  214.9 57.5 %all_to_all.21 = bf16[32,8,7168]{2,1,0:T(8,128)(2,1)S(1)} all-to-all(bf16[32,8,7168]{2,1,0:T(8,128)(2,1)S(1)} %fusion.2), channel_id=1, replica_groups=mesh['dp'=8,'expert'=32] {'expert'}, dimensions={0} | all-to-all | bytes 7340032 | tf_op jit(solution)/shard_map/all_to_all | solution.py:22
  276.4 3.0 fusion.3
  279.4 5.0 %all-to-all-start.3 = ((bf16[32,8,7168]{2,1,0:T(8,128)(2,1)}), bf16[32,8,7168]{2,1,0:T(8,128)(2,1)}, u32[]{:S(2)}, u32[]{:S(2)}) async-start(bf16[32,8,7168]{2,1,0:T(8,128)(2,1)} %fusion.3), calls=%async_computation.3 | async-start | bytes 7340032 | tf_op jit(solution)/shard_map/all_to_all | solution.py:22
  284.6 45.0 %all-to-all-done.3 = bf16[32,8,7168]{2,1,0:T(8,128)(2,1)} async-done(((bf16[32,8,7168]{2,1,0:T(8,128)(2,1)}), bf16[32,8,7168]{2,1,0:T(8,128)(2,1)}, u32[]{:S(2)}, u32[]{:S(2)}) %all-to-all-start.3) | async-done | bytes 3670048 | tf_op jit(solution)/shard_map/all_to_all | solution.py:22
  329.6 3.6 fusion.8
  337.0 2.5 collective-permute-start.12
  351.2 2.7 collective-permute-start.14
  356.9 3.3 collective-permute-start.15
  363.2 2.7 collective-permute-start.16
  365.8 3.7 collective-permute-done.16
  369.5 8.2 %collective-permute-start.17 = (f32[3]{0:T(128)S(1)}, f32[3]{0:T(128)S(1)}, u32[]{:S(2)}, u32[]{:S(2)}) collective-permute-start(f32[3]{0:T(128)S(1)} %add.224), channel_id=1, source_target_pairs={{0,1},{1,0},{2,3},{3,2},{4,5},{5,4},{6,7},{7,6},{8,9},{9,8},{10,11... | collective-permute-start | bytes 44 | tf_op jit(solution)/shard_map/ppermute | solution.py:53
  380.9 3.9 collective-permute-done.19
  388.1 3.1 collective-permute-done.21
  (107 shorter events, 50.8 us)
Async XLA Ops:
  2.9 14.9 %collective-permute-start = (bf16[2,14464]{1,0:T(2,128)(2,1)S(1)}, bf16[2,14464]{1,0:T(2,128)(2,1)S(1)}, u32[]{:S(2)}, u32[]{:S(2)}) collective-permute-start(bf16[2,14464]{1,0:T(2,128)(2,1)S(1)} %concatenate.6), channel_id=1, source_target_pairs={{0,32},{32,64},{64,96},{96,128},{128,160},{160,192},{192,224},{224... | collective-permute-start | bytes 173576 | tf_op jit(solution)/shard_map/ppermute | solution.py:26
  5.4 14.9 %collective-permute-start.1 = (bf16[2,14464]{1,0:T(2,128)(2,1)S(1)}, bf16[2,14464]{1,0:T(2,128)(2,1)S(1)}, u32[]{:S(2)}, u32[]{:S(2)}) collective-permute-start(bf16[2,14464]{1,0:T(2,128)(2,1)S(1)} %concatenate.6), channel_id=1, source_target_pairs={{0,64},{32,96},{64,128},{96,160},{128,192},{160,224},{192,0},{224,... | collective-permute-start | bytes 173576 | tf_op jit(solution)/shard_map/ppermute | solution.py:26
  8.4 12.8 %collective-permute-start.2 = (bf16[2,14464]{1,0:T(2,128)(2,1)S(1)}, bf16[2,14464]{1,0:T(2,128)(2,1)S(1)}, u32[]{:S(2)}, u32[]{:S(2)}) collective-permute-start(bf16[2,14464]{1,0:T(2,128)(2,1)S(1)} %concatenate.6), channel_id=1, source_target_pairs={{0,96},{32,128},{64,160},{96,192},{128,224},{160,0},{192,32},{224,... | collective-permute-start | bytes 173576 | tf_op jit(solution)/shard_map/ppermute | solution.py:26
  12.2 9.1 %collective-permute-start.3 = (bf16[2,14464]{1,0:T(2,128)(2,1)S(1)}, bf16[2,14464]{1,0:T(2,128)(2,1)S(1)}, u32[]{:S(2)}, u32[]{:S(2)}) collective-permute-start(bf16[2,14464]{1,0:T(2,128)(2,1)S(1)} %concatenate.6), channel_id=1, source_target_pairs={{0,128},{32,160},{64,192},{96,224},{128,0},{160,32},{192,64},{224,... | collective-permute-start | bytes 173576 | tf_op jit(solution)/shard_map/ppermute | solution.py:26
  12.6 8.7 %collective-permute-start.4 = (bf16[2,14464]{1,0:T(2,128)(2,1)S(1)}, bf16[2,14464]{1,0:T(2,128)(2,1)S(1)}, u32[]{:S(2)}, u32[]{:S(2)}) collective-permute-start(bf16[2,14464]{1,0:T(2,128)(2,1)S(1)} %concatenate.6), channel_id=1, source_target_pairs={{0,160},{32,192},{64,224},{96,0},{128,32},{160,64},{192,96},{224,1... | collective-permute-start | bytes 173576 | tf_op jit(solution)/shard_map/ppermute | solution.py:26
  17.8 8.7 %collective-permute-start.5 = (bf16[2,14464]{1,0:T(2,128)(2,1)S(1)}, bf16[2,14464]{1,0:T(2,128)(2,1)S(1)}, u32[]{:S(2)}, u32[]{:S(2)}) collective-permute-start(bf16[2,14464]{1,0:T(2,128)(2,1)S(1)} %concatenate.6), channel_id=1, source_target_pairs={{0,192},{32,224},{64,0},{96,32},{128,64},{160,96},{192,128},{224,1... | collective-permute-start | bytes 173576 | tf_op jit(solution)/shard_map/ppermute | solution.py:26
  20.4 6.2 %collective-permute-start.6 = (bf16[2,14464]{1,0:T(2,128)(2,1)S(1)}, bf16[2,14464]{1,0:T(2,128)(2,1)S(1)}, u32[]{:S(2)}, u32[]{:S(2)}) collective-permute-start(bf16[2,14464]{1,0:T(2,128)(2,1)S(1)} %concatenate.6), channel_id=1, source_target_pairs={{0,224},{32,0},{64,32},{96,64},{128,96},{160,128},{192,160},{224,1... | collective-permute-start | bytes 173576 | tf_op jit(solution)/shard_map/ppermute | solution.py:26
  131.9 50.0 %all-to-all-start.1 = ((bf16[32,8,7168]{2,1,0:T(8,128)(2,1)}), bf16[32,8,7168]{2,1,0:T(8,128)(2,1)}, u32[]{:S(2)}, u32[]{:S(2)}) async-start(bf16[32,8,7168]{2,1,0:T(8,128)(2,1)} %fusion.1), calls=%async_computation.1 | async-start | bytes 7340032 | tf_op jit(solution)/shard_map/all_to_all | solution.py:22
  279.4 50.2 %all-to-all-start.3 = ((bf16[32,8,7168]{2,1,0:T(8,128)(2,1)}), bf16[32,8,7168]{2,1,0:T(8,128)(2,1)}, u32[]{:S(2)}, u32[]{:S(2)}) async-start(bf16[32,8,7168]{2,1,0:T(8,128)(2,1)} %fusion.3), calls=%async_computation.3 | async-start | bytes 7340032 | tf_op jit(solution)/shard_map/all_to_all | solution.py:22
  333.6 7.6 %collective-permute-start.10 = (f32[2,7168]{1,0:T(2,128)S(1)}, f32[2,7168]{1,0:T(2,128)S(1)}, u32[]{:S(2)}, u32[]{:S(2)}) collective-permute-start(f32[2,7168]{1,0:T(2,128)S(1)} %bitcast.188), channel_id=1, source_target_pairs={{0,128},{32,160},{64,192},{96,224},{128,0},{160,32},{192,64},{224,... | collective-permute-start | bytes 172040 | tf_op jit(solution)/shard_map/ppermute | solution.py:26
  335.7 6.6 %collective-permute-start.11 = (f32[2,7168]{1,0:T(2,128)S(1)}, f32[2,7168]{1,0:T(2,128)S(1)}, u32[]{:S(2)}, u32[]{:S(2)}) collective-permute-start(f32[2,7168]{1,0:T(2,128)S(1)} %bitcast.186), channel_id=1, source_target_pairs={{0,160},{32,192},{64,224},{96,0},{128,32},{160,64},{192,96},{224,1... | collective-permute-start | bytes 172040 | tf_op jit(solution)/shard_map/ppermute | solution.py:26
  337.0 7.7 %collective-permute-start.12 = (f32[2,7168]{1,0:T(2,128)S(1)}, f32[2,7168]{1,0:T(2,128)S(1)}, u32[]{:S(2)}, u32[]{:S(2)}) collective-permute-start(f32[2,7168]{1,0:T(2,128)S(1)} %bitcast.185), channel_id=1, source_target_pairs={{0,192},{32,224},{64,0},{96,32},{128,64},{160,96},{192,128},{224,1... | collective-permute-start | bytes 172040 | tf_op jit(solution)/shard_map/ppermute | solution.py:26
  339.5 6.9 %collective-permute-start.13 = (f32[2,7168]{1,0:T(2,128)S(1)}, f32[2,7168]{1,0:T(2,128)S(1)}, u32[]{:S(2)}, u32[]{:S(2)}) collective-permute-start(f32[2,7168]{1,0:T(2,128)S(1)} %bitcast.187), channel_id=1, source_target_pairs={{0,224},{32,0},{64,32},{96,64},{128,96},{160,128},{192,160},{224,1... | collective-permute-start | bytes 172040 | tf_op jit(solution)/shard_map/ppermute | solution.py:26
  340.8 5.6 %collective-permute-start.7 = (f32[2,7168]{1,0:T(2,128)S(1)}, f32[2,7168]{1,0:T(2,128)S(1)}, u32[]{:S(2)}, u32[]{:S(2)}) collective-permute-start(f32[2,7168]{1,0:T(2,128)S(1)} %bitcast.189), channel_id=1, source_target_pairs={{0,32},{32,64},{64,96},{96,128},{128,160},{160,192},{192,224},{224... | collective-permute-start | bytes 172040 | tf_op jit(solution)/shard_map/ppermute | solution.py:26
  341.2 5.3 %collective-permute-start.8 = (f32[2,7168]{1,0:T(2,128)S(1)}, f32[2,7168]{1,0:T(2,128)S(1)}, u32[]{:S(2)}, u32[]{:S(2)}) collective-permute-start(f32[2,7168]{1,0:T(2,128)S(1)} %bitcast.191), channel_id=1, source_target_pairs={{0,64},{32,96},{64,128},{96,160},{128,192},{160,224},{192,0},{224,... | collective-permute-start | bytes 172040 | tf_op jit(solution)/shard_map/ppermute | solution.py:26
  342.3 6.1 %collective-permute-start.9 = (f32[2,7168]{1,0:T(2,128)S(1)}, f32[2,7168]{1,0:T(2,128)S(1)}, u32[]{:S(2)}, u32[]{:S(2)}) collective-permute-start(f32[2,7168]{1,0:T(2,128)S(1)} %bitcast.190), channel_id=1, source_target_pairs={{0,96},{32,128},{64,160},{96,192},{128,224},{160,0},{192,32},{224,... | collective-permute-start | bytes 172040 | tf_op jit(solution)/shard_map/ppermute | solution.py:26
  351.2 3.7 collective-permute-start.14
  356.9 4.2 %collective-permute-start.15 = (f32[3]{0:T(128)S(1)}, f32[3]{0:T(128)S(1)}, u32[]{:S(2)}, u32[]{:S(2)}) collective-permute-start(f32[3]{0:T(128)S(1)} %fusion.73), channel_id=1, source_target_pairs={{0,64},{32,96},{64,0},{96,32},{128,192},{160,224},{192,128},{224,1... | collective-permute-start | bytes 44 | tf_op jit(solution)/shard_map/ppermute | solution.py:53
  363.2 6.4 %collective-permute-start.16 = (f32[3]{0:T(128)S(1)}, f32[3]{0:T(128)S(1)}, u32[]{:S(2)}, u32[]{:S(2)}) collective-permute-start(f32[3]{0:T(128)S(1)} %fusion.74), channel_id=1, source_target_pairs={{0,128},{32,160},{64,192},{96,224},{128,0},{160,32},{192,64},{224,... | collective-permute-start | bytes 44 | tf_op jit(solution)/shard_map/ppermute | solution.py:53
  369.5 9.0 %collective-permute-start.17 = (f32[3]{0:T(128)S(1)}, f32[3]{0:T(128)S(1)}, u32[]{:S(2)}, u32[]{:S(2)}) collective-permute-start(f32[3]{0:T(128)S(1)} %add.224), channel_id=1, source_target_pairs={{0,1},{1,0},{2,3},{3,2},{4,5},{5,4},{6,7},{7,6},{8,9},{9,8},{10,11... | collective-permute-start | bytes 44 | tf_op jit(solution)/shard_map/ppermute | solution.py:53
  378.5 2.4 collective-permute-start.18
  380.9 3.9 collective-permute-start.19
  384.9 2.4 collective-permute-start.20
  387.3 3.9 collective-permute-start.21
  (7 other events, 222.7 us)

commit v3 on v2

--- a/solution.py
+++ b/solution.py
@@ -29,10 +29,15 @@
 def gather_rows(value, axis):
     size = lax.axis_size(axis)
     me = lax.axis_index(axis)
-    got = jnp.stack([value] + [shifted(value, axis, size, s) for s in range(1, size)])
-    source_slot = (me - jnp.arange(size)) % size
-    order = jnp.zeros((size,), jnp.int32).at[source_slot].set(jnp.arange(size))
-    return got[order].reshape(size * value.shape[0], *value.shape[1:])
+    step = 1
+    while step < size:
+        other = lax.ppermute(value, axis, [(i, i ^ step) for i in range(size)])
+        upper = (me // step) % 2 == 1
+        value = jnp.concatenate(
+            [jnp.where(upper, other, value), jnp.where(upper, value, other)], axis=0
+        )
+        step *= 2
+    return value
 
 
 def scatter_sum_rows(value, axis):
@@ -55,6 +60,12 @@
     return value
 
 
+def combine(combine_two, rows):
+    both = jnp.dot(combine_two, rows, preferred_element_type=F32)
+    half = both.shape[0] // 2
+    return both[:half] + both[half:]
+
+
 def body(tokens, tangent, route_ids, gate_fixed, gate_proj, up_proj, down_proj):
     model_width = tokens.shape[2]
     tok_dev = tokens.shape[1]
@@ -63,25 +74,20 @@
     gates_local = gate_fixed[0]
     pieces = [
         tokens[0],
-        tangent[0],
         route_ids[0].astype(BF16),
         (gates_local // 256).astype(BF16),
         (gates_local % 256).astype(BF16),
     ]
-    width = 2 * model_width + 3 * top_count
+    width = model_width + 3 * top_count
     pad = (-width) % 128
     if pad:
         pieces.append(jnp.zeros((tok_dev, pad), BF16))
-    packed = jnp.concatenate(pieces, axis=1)
-    col = gather_rows(packed, "dp")
+    col = gather_rows(jnp.concatenate(pieces, axis=1), "dp")
     col_count = col.shape[0]
-    meta = col[:, 2 * model_width: width].astype(jnp.int32)
+    meta = col[:, model_width: width].astype(jnp.int32)
     col_ids = meta[:, :top_count]
     col_gates = meta[:, top_count: 2 * top_count] * 256 + meta[:, 2 * top_count:]
-    col_pair = jnp.concatenate(
-        [col[:, :model_width], col[:, model_width: 2 * model_width]], axis=0
-    )
-
+    col_tokens = col[:, :model_width]
     capacity = min(col_count, 2 * col_count * top_count // experts)
     slot_total = experts * capacity
     flat_ids = col_ids.reshape(-1)
@@ -101,33 +107,33 @@
         jnp.where(matches, gate_vals[:, None], 0.0).reshape(col_count, top_count, slot_total),
         axis=1,
     )
-    eye2 = jnp.eye(2, dtype=F32)
-    pair_map = (
-        route_f.reshape(experts, 1, capacity, 1, col_count)
-        * eye2.reshape(1, 2, 1, 2, 1)
-    ).reshape(experts * 2 * capacity, 2 * col_count).astype(BF16)
-    send_pair = (
-        jnp.dot(pair_map, col_pair, preferred_element_type=F32)
-        .astype(BF16)
-        .reshape(experts, 2 * capacity, model_width)
-    )
+    combine_hi = combine_map.astype(BF16)
+    combine_lo = (combine_map - combine_hi.astype(F32)).astype(BF16)
+    combine_two = jnp.concatenate([combine_hi, combine_lo], axis=0)
     weight_gate = gate_proj[0]
     weight_up = up_proj[0]
     weight_down = down_proj[0]
     hidden_dev = weight_gate.shape[1]
-    rows_pair = exchange(send_pair)
-    groups_here = rows_pair.shape[0]
-    flat_pair = rows_pair.reshape(-1, model_width)
-    gate_both = jnp.dot(flat_pair, weight_gate, preferred_element_type=F32).reshape(
-        groups_here, 2, capacity, hidden_dev
+    send_in = (
+        jnp.dot(route_map, col_tokens, preferred_element_type=F32)
+        .astype(BF16)
+        .reshape(experts, capacity, model_width)
     )
-    up_both = jnp.dot(flat_pair, weight_up, preferred_element_type=F32).reshape(
-        groups_here, 2, capacity, hidden_dev
+    rows_in = exchange(send_in)
+    col_tangent = gather_rows(tangent[0], "dp")
+    send_dir = (
+        jnp.dot(route_map, col_tangent, preferred_element_type=F32)
+        .astype(BF16)
+        .reshape(experts, capacity, model_width)
     )
-    gate_pre = gate_both[:, 0].reshape(-1, hidden_dev)
-    gate_dir = gate_both[:, 1].reshape(-1, hidden_dev)
-    up_pre = up_both[:, 0].reshape(-1, hidden_dev)
-    up_dir = up_both[:, 1].reshape(-1, hidden_dev)
+    rows_dir = exchange(send_dir)
+    groups_here = rows_in.shape[0]
+    flat_in = rows_in.reshape(-1, model_width)
+    flat_dir = rows_dir.reshape(-1, model_width)
+    gate_pre = jnp.dot(flat_in, weight_gate, preferred_element_type=F32)
+    up_pre = jnp.dot(flat_in, weight_up, preferred_element_type=F32)
+    gate_dir = jnp.dot(flat_dir, weight_gate, preferred_element_type=F32)
+    up_dir = jnp.dot(flat_dir, weight_up, preferred_element_type=F32)
     silu_value, silu_slope = silu_parts(gate_pre)
     jvp_hidden = (silu_slope * gate_dir * up_pre + silu_value * up_dir).astype(BF16)
     partial_value = jnp.dot(jvp_hidden, weight_down, preferred_element_type=F32)
@@ -136,12 +142,7 @@
     )
     gate_coef = silu_slope * up_pre
     up_coef = silu_value
-    product_part = jnp.dot(
-        combine_map,
-        returned.reshape(slot_total, -1).astype(F32),
-        precision=lax.Precision.HIGHEST,
-        preferred_element_type=F32,
-    )
+    product_part = combine(combine_two, returned.reshape(slot_total, -1))
     product_bf = lax.psum(product_part, "dp").astype(BF16)
     send_prod = (
         jnp.dot(route_map, product_bf, preferred_element_type=F32)
@@ -156,12 +157,7 @@
     returned_two = exchange(
         vjp_part.astype(BF16).reshape(experts, capacity, model_width)
     )
-    result_part = jnp.dot(
-        combine_map,
-        returned_two.reshape(slot_total, -1).astype(F32),
-        precision=lax.Precision.HIGHEST,
-        preferred_element_type=F32,
-    )
+    result_part = combine(combine_two, returned_two.reshape(slot_total, -1))
     result = scatter_sum_rows(result_part, "dp")
     probe_f = tangent[0].astype(F32)
     sums = jnp.stack(

time: 400 us -> 419 us (1.048)
  blocking collectives: 179 us -> 86.9 us
  waiting for transfers between devices: 117 us -> 193 us
  starting transfers between devices: 55.8 us -> 76.6 us
  matrix products: 22.8 us -> 39.9 us
    all_to_all x2 -> x1, blocking collectives: 150 us -> 57.6 us  [exchange(): lax.all_to_all(value, 'expert', split_axis=0, concat_axis=0, tiled=True)]
    all_to_all x2 -> x4, waiting for transfers between devices: 90 us -> 161 us  [exchange(): lax.all_to_all(value, 'expert', split_axis=0, concat_axis=0, tiled=True)]
    all_to_all x2 -> x4, starting transfers between devices: 9.83 us -> 32.2 us  [exchange(): lax.all_to_all(value, 'expert', split_axis=0, concat_axis=0, tiled=True)]
    ppermute x0 -> x6, starting transfers between devices: none -> 17.9 us  [gather_rows(): other = lax.ppermute(value, axis, [(i, i ^ step) for i in range(size)])]
    ppermute x14 -> x7, starting transfers between devices: 28.3 us -> 11.6 us  [shifted(): lax.ppermute(value, axis, [(i, (i + step) % size) for i in range(size)])]
    dot_general x5 -> x7, matrix products: 13.3 us -> 23.4 us  [the longest x2 5.53 us: combine(): both = jnp.dot(combine_two, rows, preferred_element_type=F32)]
    ppermute x0 -> x6, waiting for transfers between devices: none -> 7.13 us  [gather_rows(): other = lax.ppermute(value, axis, [(i, i ^ step) for i in range(size)])]
    dot_general x1, matrix products: 3.06 us -> 9.99 us  [body(): partial_value = jnp.dot(jvp_hidden, weight_down, preferred_element_type=F32)]
  transfers between devices with their start and end apart: 24 -> 25, of which waited for: 14 -> 18; matrix products, arithmetic and copies ran while one was open for 0% -> 4% of each run, Pallas kernels for 0% -> 0%
where the time goes in v3:
time: 419 us; the launch traced here: 415 us
  waiting for transfers between devices  193 us (46%)
  blocking collectives  86.9 us (21%)
  starting transfers between devices  76.6 us (18%)
  matrix products  39.9 us (10%)
  other arithmetic  11.2 us (3%)
  between operations  4.19 us (1%)
    all_to_all x4, waiting for transfers between devices, exchange(): lax.all_to_all(value, 'expert', split_axis=0, concat_axis=0, tiled=True)  161 us
    all_to_all x1, blocking collectives, exchange(): lax.all_to_all(value, 'expert', split_axis=0, concat_axis=0, tiled=True)  57.6 us
    all_to_all x4, starting transfers between devices, exchange(): lax.all_to_all(value, 'expert', split_axis=0, concat_axis=0, tiled=True)  32.2 us
    psum x1, blocking collectives, body(): product_bf = lax.psum(product_part, 'dp').astype(BF16)  29.3 us
    ppermute x8, waiting for transfers between devices, butterfly_sum(): lax.ppermute(value, axis, [(i, i ^ step) for i in range(size)])  20.3 us
    ppermute x6, starting transfers between devices, gather_rows(): other = lax.ppermute(value, axis, [(i, i ^ step) for i in range(size)])  17.9 us
    ppermute x8, starting transfers between devices, butterfly_sum(): lax.ppermute(value, axis, [(i, i ^ step) for i in range(size)])  14.9 us
    ppermute x7, starting transfers between devices, shifted(): lax.ppermute(value, axis, [(i, (i + step) % size) for i in range(size)])  11.6 us
  transfers between devices with their start and end apart: 25, of which 18 were waited for; matrix products, arithmetic and copies ran while one was open for 4% of the time, Pallas kernels for 0%

profile of v3, /device:TPU:1, one launch (start us, length us, event | category | flops | bytes accessed | tf_op | source)
XLA Modules:
  0.0 415.3 jit_solution(10335365500349436930)
XLA Ops:
  6.8 3.1 collective-permute-start.1
  11.6 6.8 %collective-permute-start.2 = (bf16[8,7296]{1,0:T(8,128)(2,1)S(1)}, bf16[8,7296]{1,0:T(8,128)(2,1)S(1)}, u32[]{:S(2)}, u32[]{:S(2)}) collective-permute-start(bf16[8,7296]{1,0:T(8,128)(2,1)S(1)} %pad_maximum_fusion.2), channel_id=1, source_target_pairs={{0,128},{32,160},{64,192},{96,224},{128,0},{160,32},{192,64},{224,... | collective-permute-start | bytes 350216 | tf_op jit(solution)/shard_map/ppermute | solution.py:34
  24.5 12.5 %all-to-all-start = ((bf16[32,8,7168]{2,1,0:T(8,128)(2,1)}), bf16[32,8,7168]{2,1,0:T(8,128)(2,1)}, u32[]{:S(2)}, u32[]{:S(2)}) async-start(bf16[32,8,7168]{2,1,0:T(8,128)(2,1)} %fusion.1), calls=%async_computation | async-start | bytes 7340032 | tf_op jit(solution)/shard_map/all_to_all | solution.py:22
  37.2 4.6 %collective-permute-start.5 = (bf16[8,7168]{1,0:T(8,128)(2,1)S(1)}, bf16[8,7168]{1,0:T(8,128)(2,1)S(1)}, u32[]{:S(2)}, u32[]{:S(2)}) collective-permute-start(bf16[8,7168]{1,0:T(8,128)(2,1)S(1)} %pad_maximum_fusion.3), channel_id=1, source_target_pairs={{0,128},{32,160},{64,192},{96,224},{128,0},{160,32},{192,64},{224,... | collective-permute-start | bytes 344072 | tf_op jit(solution)/shard_map/ppermute | solution.py:34
  41.8 3.8 collective-permute-done.5
  48.8 33.6 %all-to-all-done = bf16[32,8,7168]{2,1,0:T(8,128)(2,1)} async-done(((bf16[32,8,7168]{2,1,0:T(8,128)(2,1)}), bf16[32,8,7168]{2,1,0:T(8,128)(2,1)}, u32[]{:S(2)}, u32[]{:S(2)}) %all-to-all-start) | async-done | bytes 3670048 | tf_op jit(solution)/shard_map/all_to_all | solution.py:22
  82.4 7.3 %all-to-all-start.1 = ((bf16[32,8,7168]{2,1,0:T(8,128)(2,1)}), bf16[32,8,7168]{2,1,0:T(8,128)(2,1)}, u32[]{:S(2)}, u32[]{:S(2)}) async-start(bf16[32,8,7168]{2,1,0:T(8,128)(2,1)} %fusion.2), calls=%async_computation.1 | async-start | bytes 7340032 | tf_op jit(solution)/shard_map/all_to_all | solution.py:22
  89.7 4.4 %fusion.25 = f32[256,256]{1,0:T(8,128)S(1)} fusion(bf16[1,7168,256]{2,1,0:T(8,128)(2,1)} %param.11, bf16[32,8,7168]{2,1,0:T(8,128)(2,1)} %all-to-all-done), kind=kOutput, calls=%fused_computation.30 | convolution fusion | flops 939524096 | bytes 7602176 | tf_op jit(solution)/shard_map/dot_general | solution.py:133
  94.1 3.2 fusion.17
  97.3 37.5 %all-to-all-done.1 = bf16[32,8,7168]{2,1,0:T(8,128)(2,1)} async-done(((bf16[32,8,7168]{2,1,0:T(8,128)(2,1)}), bf16[32,8,7168]{2,1,0:T(8,128)(2,1)}, u32[]{:S(2)}, u32[]{:S(2)}) %all-to-all-start.1) | async-done | bytes 3670048 | tf_op jit(solution)/shard_map/all_to_all | solution.py:22
  134.8 4.3 %fusion.44 = f32[256,256]{1,0:T(8,128)S(1)} fusion(bf16[1,7168,256]{2,1,0:T(8,128)(2,1)} %param.12, bf16[32,8,7168]{2,1,0:T(8,128)(2,1)} %all-to-all-done.1, f32[256,256]{1,0:T(8,128)S(1)} %fusion.25), kind=kOutput, calls=%fused_computation.37 | convolution fusion | flops 939851776 | bytes 7864320 | tf_op jit(solution)/shard_map/dot_general | solution.py:136
  139.1 10.0 %fusion.3 = bf16[32,8,7168]{2,1,0:T(8,128)(2,1)} fusion(bf16[1,256,7168]{2,1,0:T(8,128)(2,1)} %param.13, f32[256,256]{1,0:T(8,128)S(1)} %fusion.44, f32[256,256]{1,0:T(8,128)S(1)} %fusion.17, bf16[1,7168,256]{2,1,0:T(8,128)(2,1)} %param.11, bf16[32,8,7168]{2,1,0:T(8,128)(2,1)} %all-to-all-done.1, f32[256,256]{1,0:T(8,128)S(1)} %fusion.25), kind=kOutput, calls=%fused_computation.8 | convolution fusion | flops 1881604096 | bytes 15466496 | tf_op jit(solution)/shard_map/dot_general | solution.py:139
  149.1 7.6 %all-to-all-start.2 = ((bf16[32,8,7168]{2,1,0:T(8,128)(2,1)}), bf16[32,8,7168]{2,1,0:T(8,128)(2,1)}, u32[]{:S(2)}, u32[]{:S(2)}) async-start(bf16[32,8,7168]{2,1,0:T(8,128)(2,1)} %fusion.3), calls=%async_computation.2 | async-start | bytes 7340032 | tf_op jit(solution)/shard_map/all_to_all | solution.py:22
  156.9 44.9 %all-to-all-done.2 = bf16[32,8,7168]{2,1,0:T(8,128)(2,1)} async-done(((bf16[32,8,7168]{2,1,0:T(8,128)(2,1)}), bf16[32,8,7168]{2,1,0:T(8,128)(2,1)}, u32[]{:S(2)}, u32[]{:S(2)}) %all-to-all-start.2) | async-done | bytes 3670048 | tf_op jit(solution)/shard_map/all_to_all | solution.py:22
  204.7 29.3 %all-reduce.1 = bf16[16,7168]{1,0:T(8,128)(2,1)S(1)} all-reduce(f32[16,7168]{1,0:T(8,128)S(1)} %slice_add_fusion.1), channel_id=1, replica_groups=mesh['dp'=8,'expert'=32] {'dp'}, use_global_device_ids=true, to_apply=%region_4.5 | all-reduce | flops 114688 | bytes 688128 | tf_op jit(solution)/shard_map/psum | solution.py:146
  235.2 57.6 %all_to_all.25 = bf16[32,8,7168]{2,1,0:T(8,128)(2,1)S(1)} all-to-all(bf16[32,8,7168]{2,1,0:T(8,128)(2,1)S(1)} %fusion.4), channel_id=1, replica_groups=mesh['dp'=8,'expert'=32] {'expert'}, dimensions={0} | all-to-all | bytes 7340032 | tf_op jit(solution)/shard_map/all_to_all | solution.py:22
  299.8 4.8 %all-to-all-start.4 = ((bf16[32,8,7168]{2,1,0:T(8,128)(2,1)}), bf16[32,8,7168]{2,1,0:T(8,128)(2,1)}, u32[]{:S(2)}, u32[]{:S(2)}) async-start(bf16[32,8,7168]{2,1,0:T(8,128)(2,1)} %fusion.5), calls=%async_computation.4 | async-start | bytes 7340032 | tf_op jit(solution)/shard_map/all_to_all | solution.py:22
  304.8 45.0 %all-to-all-done.4 = bf16[32,8,7168]{2,1,0:T(8,128)(2,1)} async-done(((bf16[32,8,7168]{2,1,0:T(8,128)(2,1)}), bf16[32,8,7168]{2,1,0:T(8,128)(2,1)}, u32[]{:S(2)}, u32[]{:S(2)}) %all-to-all-start.4) | async-done | bytes 3670048 | tf_op jit(solution)/shard_map/all_to_all | solution.py:22
  361.4 3.3 collective-permute-start.9
  365.1 3.7 collective-permute-done.9
  376.3 3.9 collective-permute-start.14
  385.0 4.6 %collective-permute-done.15 = f32[3]{0:T(128)S(1)} collective-permute-done((f32[3]{0:T(128)S(1)}, f32[3]{0:T(128)S(1)}, u32[]{:S(2)}, u32[]{:S(2)}) %collective-permute-start.15) | collective-permute-done | bytes 44 | tf_op jit(solution)/shard_map/ppermute | solution.py:58
  389.5 7.8 %collective-permute-start.16 = (f32[3]{0:T(128)S(1)}, f32[3]{0:T(128)S(1)}, u32[]{:S(2)}, u32[]{:S(2)}) collective-permute-start(f32[3]{0:T(128)S(1)} %add.212), channel_id=1, source_target_pairs={{0,1},{1,0},{2,3},{3,2},{4,5},{5,4},{6,7},{7,6},{8,9},{9,8},{10,11... | collective-permute-start | bytes 44 | tf_op jit(solution)/shard_map/ppermute | solution.py:58
  400.6 3.9 collective-permute-done.18
  (91 shorter events, 63.6 us)
Async XLA Ops:
  2.8 3.8 collective-permute-start
  5.4 4.5 %collective-permute-start.3 = (bf16[2,7168]{1,0:T(2,128)(2,1)}, bf16[2,7168]{1,0:T(2,128)(2,1)S(1)}, u32[]{:S(2)}, u32[]{:S(2)}) collective-permute-start(bf16[2,7168]{1,0:T(2,128)(2,1)} %bitcast.141), channel_id=1, source_target_pairs={{0,32},{32,0},{64,96},{96,64},{128,160},{160,128},{192,224},{224,1... | collective-permute-start | bytes 86024 | tf_op jit(solution)/shard_map/ppermute | solution.py:34
  6.8 4.7 %collective-permute-start.1 = (bf16[4,7296]{1,0:T(4,128)(2,1)S(1)}, bf16[4,7296]{1,0:T(4,128)(2,1)S(1)}, u32[]{:S(2)}, u32[]{:S(2)}) collective-permute-start(bf16[4,7296]{1,0:T(4,128)(2,1)S(1)} %pad_maximum_fusion.4), channel_id=1, source_target_pairs={{0,64},{32,96},{64,0},{96,32},{128,192},{160,224},{192,128},{224,1... | collective-permute-start | bytes 175112 | tf_op jit(solution)/shard_map/ppermute | solution.py:34
  11.6 9.0 %collective-permute-start.2 = (bf16[8,7296]{1,0:T(8,128)(2,1)S(1)}, bf16[8,7296]{1,0:T(8,128)(2,1)S(1)}, u32[]{:S(2)}, u32[]{:S(2)}) collective-permute-start(bf16[8,7296]{1,0:T(8,128)(2,1)S(1)} %pad_maximum_fusion.2), channel_id=1, source_target_pairs={{0,128},{32,160},{64,192},{96,224},{128,0},{160,32},{192,64},{224,... | collective-permute-start | bytes 350216 | tf_op jit(solution)/shard_map/ppermute | solution.py:34
  18.5 18.5 %collective-permute-start.4 = (bf16[4,7168]{1,0:T(4,128)(2,1)S(1)}, bf16[4,7168]{1,0:T(4,128)(2,1)S(1)}, u32[]{:S(2)}, u32[]{:S(2)}) collective-permute-start(bf16[4,7168]{1,0:T(4,128)(2,1)S(1)} %pad_maximum_fusion.5), channel_id=1, source_target_pairs={{0,64},{32,96},{64,0},{96,32},{128,192},{160,224},{192,128},{224,1... | collective-permute-start | bytes 172040 | tf_op jit(solution)/shard_map/ppermute | solution.py:34
  24.5 57.9 %all-to-all-start = ((bf16[32,8,7168]{2,1,0:T(8,128)(2,1)}), bf16[32,8,7168]{2,1,0:T(8,128)(2,1)}, u32[]{:S(2)}, u32[]{:S(2)}) async-start(bf16[32,8,7168]{2,1,0:T(8,128)(2,1)} %fusion.1), calls=%async_computation | async-start | bytes 7340032 | tf_op jit(solution)/shard_map/all_to_all | solution.py:22
  37.2 8.4 %collective-permute-start.5 = (bf16[8,7168]{1,0:T(8,128)(2,1)S(1)}, bf16[8,7168]{1,0:T(8,128)(2,1)S(1)}, u32[]{:S(2)}, u32[]{:S(2)}) collective-permute-start(bf16[8,7168]{1,0:T(8,128)(2,1)S(1)} %pad_maximum_fusion.3), channel_id=1, source_target_pairs={{0,128},{32,160},{64,192},{96,224},{128,0},{160,32},{192,64},{224,... | collective-permute-start | bytes 344072 | tf_op jit(solution)/shard_map/ppermute | solution.py:34
  82.4 52.4 %all-to-all-start.1 = ((bf16[32,8,7168]{2,1,0:T(8,128)(2,1)}), bf16[32,8,7168]{2,1,0:T(8,128)(2,1)}, u32[]{:S(2)}, u32[]{:S(2)}) async-start(bf16[32,8,7168]{2,1,0:T(8,128)(2,1)} %fusion.2), calls=%async_computation.1 | async-start | bytes 7340032 | tf_op jit(solution)/shard_map/all_to_all | solution.py:22
  149.1 52.8 %all-to-all-start.2 = ((bf16[32,8,7168]{2,1,0:T(8,128)(2,1)}), bf16[32,8,7168]{2,1,0:T(8,128)(2,1)}, u32[]{:S(2)}, u32[]{:S(2)}) async-start(bf16[32,8,7168]{2,1,0:T(8,128)(2,1)} %fusion.3), calls=%async_computation.2 | async-start | bytes 7340032 | tf_op jit(solution)/shard_map/all_to_all | solution.py:22
  299.8 50.0 %all-to-all-start.4 = ((bf16[32,8,7168]{2,1,0:T(8,128)(2,1)}), bf16[32,8,7168]{2,1,0:T(8,128)(2,1)}, u32[]{:S(2)}, u32[]{:S(2)}) async-start(bf16[32,8,7168]{2,1,0:T(8,128)(2,1)} %fusion.5), calls=%async_computation.4 | async-start | bytes 7340032 | tf_op jit(solution)/shard_map/all_to_all | solution.py:22
  353.0 6.0 %collective-permute-start.10 = (f32[2,7168]{1,0:T(2,128)S(1)}, f32[2,7168]{1,0:T(2,128)S(1)}, u32[]{:S(2)}, u32[]{:S(2)}) collective-permute-start(f32[2,7168]{1,0:T(2,128)S(1)} %get-tuple-element.9), channel_id=1, source_target_pairs={{0,160},{32,192},{64,224},{96,0},{128,32},{160,64},{192,96},{224,1... | collective-permute-start | bytes 172040 | tf_op jit(solution)/shard_map/ppermute | solution.py:26
  353.9 7.5 %collective-permute-start.11 = (f32[2,7168]{1,0:T(2,128)S(1)}, f32[2,7168]{1,0:T(2,128)S(1)}, u32[]{:S(2)}, u32[]{:S(2)}) collective-permute-start(f32[2,7168]{1,0:T(2,128)S(1)} %get-tuple-element.8), channel_id=1, source_target_pairs={{0,192},{32,224},{64,0},{96,32},{128,64},{160,96},{192,128},{224,1... | collective-permute-start | bytes 172040 | tf_op jit(solution)/shard_map/ppermute | solution.py:26
  356.3 8.4 %collective-permute-start.12 = (f32[2,7168]{1,0:T(2,128)S(1)}, f32[2,7168]{1,0:T(2,128)S(1)}, u32[]{:S(2)}, u32[]{:S(2)}) collective-permute-start(f32[2,7168]{1,0:T(2,128)S(1)} %get-tuple-element.7), channel_id=1, source_target_pairs={{0,224},{32,0},{64,32},{96,64},{128,96},{160,128},{192,160},{224,1... | collective-permute-start | bytes 172040 | tf_op jit(solution)/shard_map/ppermute | solution.py:26
  357.8 6.9 %collective-permute-start.6 = (f32[2,7168]{1,0:T(2,128)S(1)}, f32[2,7168]{1,0:T(2,128)S(1)}, u32[]{:S(2)}, u32[]{:S(2)}) collective-permute-start(f32[2,7168]{1,0:T(2,128)S(1)} %get-tuple-element.6), channel_id=1, source_target_pairs={{0,32},{32,64},{64,96},{96,128},{128,160},{160,192},{192,224},{224... | collective-permute-start | bytes 172040 | tf_op jit(solution)/shard_map/ppermute | solution.py:26
  357.8 6.9 %collective-permute-start.7 = (f32[2,7168]{1,0:T(2,128)S(1)}, f32[2,7168]{1,0:T(2,128)S(1)}, u32[]{:S(2)}, u32[]{:S(2)}) collective-permute-start(f32[2,7168]{1,0:T(2,128)S(1)} %get-tuple-element.12), channel_id=1, source_target_pairs={{0,64},{32,96},{64,128},{96,160},{128,192},{160,224},{192,0},{224,... | collective-permute-start | bytes 172040 | tf_op jit(solution)/shard_map/ppermute | solution.py:26
  359.0 6.1 %collective-permute-start.8 = (f32[2,7168]{1,0:T(2,128)S(1)}, f32[2,7168]{1,0:T(2,128)S(1)}, u32[]{:S(2)}, u32[]{:S(2)}) collective-permute-start(f32[2,7168]{1,0:T(2,128)S(1)} %get-tuple-element.11), channel_id=1, source_target_pairs={{0,96},{32,128},{64,160},{96,192},{128,224},{160,0},{192,32},{224,... | collective-permute-start | bytes 172040 | tf_op jit(solution)/shard_map/ppermute | solution.py:26
  361.4 7.5 %collective-permute-start.9 = (f32[2,7168]{1,0:T(2,128)S(1)}, f32[2,7168]{1,0:T(2,128)S(1)}, u32[]{:S(2)}, u32[]{:S(2)}) collective-permute-start(f32[2,7168]{1,0:T(2,128)S(1)} %get-tuple-element.10), channel_id=1, source_target_pairs={{0,128},{32,160},{64,192},{96,224},{128,0},{160,32},{192,64},{224,... | collective-permute-start | bytes 172040 | tf_op jit(solution)/shard_map/ppermute | solution.py:26
  371.6 2.7 collective-permute-start.13
  376.3 4.9 %collective-permute-start.14 = (f32[3]{0:T(128)S(1)}, f32[3]{0:T(128)S(1)}, u32[]{:S(2)}, u32[]{:S(2)}) collective-permute-start(f32[3]{0:T(128)S(1)} %fusion.88), channel_id=1, source_target_pairs={{0,64},{32,96},{64,0},{96,32},{128,192},{160,224},{192,128},{224,1... | collective-permute-start | bytes 44 | tf_op jit(solution)/shard_map/ppermute | solution.py:58
  383.2 6.4 %collective-permute-start.15 = (f32[3]{0:T(128)S(1)}, f32[3]{0:T(128)S(1)}, u32[]{:S(2)}, u32[]{:S(2)}) collective-permute-start(f32[3]{0:T(128)S(1)} %fusion.89), channel_id=1, source_target_pairs={{0,128},{32,160},{64,192},{96,224},{128,0},{160,32},{192,64},{224,... | collective-permute-start | bytes 44 | tf_op jit(solution)/shard_map/ppermute | solution.py:58
  389.5 8.6 %collective-permute-start.16 = (f32[3]{0:T(128)S(1)}, f32[3]{0:T(128)S(1)}, u32[]{:S(2)}, u32[]{:S(2)}) collective-permute-start(f32[3]{0:T(128)S(1)} %add.212), channel_id=1, source_target_pairs={{0,1},{1,0},{2,3},{3,2},{4,5},{5,4},{6,7},{7,6},{8,9},{9,8},{10,11... | collective-permute-start | bytes 44 | tf_op jit(solution)/shard_map/ppermute | solution.py:58
  398.2 2.4 collective-permute-start.17
  400.6 3.9 collective-permute-start.18
  406.9 3.9 collective-permute-start.20
  (6 other events, 132.6 us)

commit v4 on v2

--- a/solution.py
+++ b/solution.py
@@ -29,10 +29,15 @@
 def gather_rows(value, axis):
     size = lax.axis_size(axis)
     me = lax.axis_index(axis)
-    got = jnp.stack([value] + [shifted(value, axis, size, s) for s in range(1, size)])
-    source_slot = (me - jnp.arange(size)) % size
-    order = jnp.zeros((size,), jnp.int32).at[source_slot].set(jnp.arange(size))
-    return got[order].reshape(size * value.shape[0], *value.shape[1:])
+    step = 1
+    while step < size:
+        other = lax.ppermute(value, axis, [(i, i ^ step) for i in range(size)])
+        upper = (me // step) % 2 == 1
+        value = jnp.concatenate(
+            [jnp.where(upper, other, value), jnp.where(upper, value, other)], axis=0
+        )
+        step *= 2
+    return value
 
 
 def scatter_sum_rows(value, axis):
@@ -53,6 +58,12 @@
         value = value + lax.ppermute(value, axis, [(i, i ^ step) for i in range(size)])
         step *= 2
     return value
+
+
+def combine(combine_two, rows):
+    both = jnp.dot(combine_two, rows, preferred_element_type=F32)
+    half = both.shape[0] // 2
+    return both[:half] + both[half:]
 
 
 def body(tokens, tangent, route_ids, gate_fixed, gate_proj, up_proj, down_proj):
@@ -101,6 +112,10 @@
         jnp.where(matches, gate_vals[:, None], 0.0).reshape(col_count, top_count, slot_total),
         axis=1,
     )
+    combine_hi = lax.reduce_precision(combine_map, exponent_bits=8, mantissa_bits=7)
+    combine_two = jnp.concatenate(
+        [combine_hi.astype(BF16), (combine_map - combine_hi).astype(BF16)], axis=0
+    )
     eye2 = jnp.eye(2, dtype=F32)
     pair_map = (
         route_f.reshape(experts, 1, capacity, 1, col_count)
@@ -136,12 +151,7 @@
     )
     gate_coef = silu_slope * up_pre
     up_coef = silu_value
-    product_part = jnp.dot(
-        combine_map,
-        returned.reshape(slot_total, -1).astype(F32),
-        precision=lax.Precision.HIGHEST,
-        preferred_element_type=F32,
-    )
+    product_part = combine(combine_two, returned.reshape(slot_total, -1))
     product_bf = lax.psum(product_part, "dp").astype(BF16)
     send_prod = (
         jnp.dot(route_map, product_bf, preferred_element_type=F32)
@@ -156,19 +166,22 @@
     returned_two = exchange(
         vjp_part.astype(BF16).reshape(experts, capacity, model_width)
     )
-    result_part = jnp.dot(
-        combine_map,
-        returned_two.reshape(slot_total, -1).astype(F32),
-        precision=lax.Precision.HIGHEST,
-        preferred_element_type=F32,
-    )
+    result_part = combine(combine_two, returned_two.reshape(slot_total, -1))
     result = scatter_sum_rows(result_part, "dp")
     probe_f = tangent[0].astype(F32)
-    sums = jnp.stack(
-        [jnp.sum(probe_f * result), jnp.sum(result * result), jnp.sum(probe_f * probe_f)]
-    )
+    lane = jnp.arange(128)[None, :]
+    row = jnp.arange(8)[:, None] == 0
+    sums = jnp.where(
+        row & (lane == 0),
+        jnp.sum(probe_f * result),
+        jnp.where(
+            row & (lane == 1),
+            jnp.sum(result * result),
+            jnp.where(row & (lane == 2), jnp.sum(probe_f * probe_f), 0.0),
+        ),
+    ).astype(F32)
     sums = butterfly_sum(butterfly_sum(sums, "dp"), "expert")
-    probe_result, result_sq, probe_sq = sums[0], sums[1], sums[2]
+    probe_result, result_sq, probe_sq = sums[0, 0], sums[0, 1], sums[0, 2]
     total_cells = lax.axis_size("dp") * lax.axis_size("expert") * tok_dev * model_width
     next_tangent = (result * lax.rsqrt(result_sq / total_cells + 1e-06)).astype(BF16)
     lipschitz = jnp.sqrt(probe_result / probe_sq)

time: 400 us -> 401 us (level)
  blocking collectives: 179 us -> 187 us
    ppermute x14 -> x7, starting transfers between devices: 28.3 us -> 12.6 us  [shifted(): lax.ppermute(value, axis, [(i, (i + step) % size) for i in range(size)])]
    ppermute x0 -> x3, starting transfers between devices: none -> 13.5 us  [gather_rows(): other = lax.ppermute(value, axis, [(i, i ^ step) for i in range(size)])]
    ppermute x0 -> x3, waiting for transfers between devices: none -> 7.31 us  [gather_rows(): other = lax.ppermute(value, axis, [(i, i ^ step) for i in range(size)])]
    ppermute x14 -> x7, waiting for transfers between devices: 8.95 us -> 4.03 us  [shifted(): lax.ppermute(value, axis, [(i, (i + step) % size) for i in range(size)])]
    all_to_all x2, blocking collectives: 150 us -> 155 us  [exchange(): lax.all_to_all(value, 'expert', split_axis=0, concat_axis=0, tiled=True)]
  transfers between devices with their start and end apart: 24 -> 20, of which waited for: 14 -> 15; matrix products, arithmetic and copies ran while one was open for 0% -> 0% of each run, Pallas kernels for 0% -> 0%
where the time goes in v4:
time: 401 us; the launch traced here: 397 us
  blocking collectives  187 us (47%)
  waiting for transfers between devices  118 us (29%)
  starting transfers between devices  52.8 us (13%)
  matrix products  21.3 us (5%)
  other arithmetic  10.7 us (3%)
  between operations  4.22 us (1%)
  local copies, waits for them, and re-layouts  4.01 us (1%)
    all_to_all x2, blocking collectives, exchange(): lax.all_to_all(value, 'expert', split_axis=0, concat_axis=0, tiled=True)  155 us
    all_to_all x2, waiting for transfers between devices, exchange(): lax.all_to_all(value, 'expert', split_axis=0, concat_axis=0, tiled=True)  90 us
    psum x1, blocking collectives, body(): product_bf = lax.psum(product_part, 'dp').astype(BF16)  32.2 us
    ppermute x8, starting transfers between devices, butterfly_sum(): lax.ppermute(value, axis, [(i, i ^ step) for i in range(size)])  17 us
    ppermute x8, waiting for transfers between devices, butterfly_sum(): lax.ppermute(value, axis, [(i, i ^ step) for i in range(size)])  16.4 us
    ppermute x3, starting transfers between devices, gather_rows(): other = lax.ppermute(value, axis, [(i, i ^ step) for i in range(size)])  13.5 us
    ppermute x7, starting transfers between devices, shifted(): lax.ppermute(value, axis, [(i, (i + step) % size) for i in range(size)])  12.6 us
    all_to_all x2, starting transfers between devices, exchange(): lax.all_to_all(value, 'expert', split_axis=0, concat_axis=0, tiled=True)  9.64 us
  transfers between devices with their start and end apart: 20, of which 15 were waited for; matrix products, arithmetic and copies ran while one was open for 0% of the time, Pallas kernels for 0%

profile of v4, /device:TPU:1, one launch (start us, length us, event | category | flops | bytes accessed | tf_op | source)
XLA Modules:
  0.0 397.5 jit_solution(3360585743193065221)
XLA Ops:
  2.9 2.5 collective-permute-start
  7.2 3.1 collective-permute-start.1
  12.8 7.9 %collective-permute-start.2 = (bf16[8,14464]{1,0:T(8,128)(2,1)S(1)}, bf16[8,14464]{1,0:T(8,128)(2,1)S(1)}, u32[]{:S(2)}, u32[]{:S(2)}) collective-permute-start(bf16[8,14464]{1,0:T(8,128)(2,1)S(1)} %pad_maximum_fusion.3), channel_id=1, source_target_pairs={{0,128},{32,160},{64,192},{96,224},{128,0},{160,32},{192,64},{224,... | collective-permute-start | bytes 694280 | tf_op jit(solution)/shard_map/ppermute | solution.py:34
  20.8 3.5 collective-permute-done.2
  27.8 97.4 %all_to_all.20 = bf16[32,16,7168]{2,1,0:T(8,128)(2,1)S(1)} all-to-all(bf16[32,16,7168]{2,1,0:T(8,128)(2,1)S(1)} %bitcast.150), channel_id=1, replica_groups=mesh['dp'=8,'expert'=32] {'expert'}, dimensions={0} | all-to-all | bytes 14680064 | tf_op jit(solution)/shard_map/all_to_all | solution.py:22
  129.4 3.1 fusion.1
  132.5 4.8 %all-to-all-start.1 = ((bf16[32,8,7168]{2,1,0:T(8,128)(2,1)}), bf16[32,8,7168]{2,1,0:T(8,128)(2,1)}, u32[]{:S(2)}, u32[]{:S(2)}) async-start(bf16[32,8,7168]{2,1,0:T(8,128)(2,1)} %fusion.1), calls=%async_computation.1 | async-start | bytes 7340032 | tf_op jit(solution)/shard_map/all_to_all | solution.py:22
  137.5 44.9 %all-to-all-done.1 = bf16[32,8,7168]{2,1,0:T(8,128)(2,1)} async-done(((bf16[32,8,7168]{2,1,0:T(8,128)(2,1)}), bf16[32,8,7168]{2,1,0:T(8,128)(2,1)}, u32[]{:S(2)}, u32[]{:S(2)}) %all-to-all-start.1) | async-done | bytes 3670048 | tf_op jit(solution)/shard_map/all_to_all | solution.py:22
  182.5 2.8 fusion.14
  185.3 32.2 %all-reduce.1 = bf16[16,7168]{1,0:T(8,128)(2,1)S(1)} all-reduce(f32[16,7168]{1,0:T(8,128)S(1)} %slice_add_fusion.1), channel_id=1, replica_groups=mesh['dp'=8,'expert'=32] {'dp'}, use_global_device_ids=true, to_apply=%region_4.5 | all-reduce | flops 114688 | bytes 688128 | tf_op jit(solution)/shard_map/psum | solution.py:155
  218.7 57.2 %all_to_all.21 = bf16[32,8,7168]{2,1,0:T(8,128)(2,1)S(1)} all-to-all(bf16[32,8,7168]{2,1,0:T(8,128)(2,1)S(1)} %fusion.2), channel_id=1, replica_groups=mesh['dp'=8,'expert'=32] {'expert'}, dimensions={0} | all-to-all | bytes 7340032 | tf_op jit(solution)/shard_map/all_to_all | solution.py:22
  279.9 3.0 fusion.3
  282.9 4.8 %all-to-all-start.3 = ((bf16[32,8,7168]{2,1,0:T(8,128)(2,1)}), bf16[32,8,7168]{2,1,0:T(8,128)(2,1)}, u32[]{:S(2)}, u32[]{:S(2)}) async-start(bf16[32,8,7168]{2,1,0:T(8,128)(2,1)} %fusion.3), calls=%async_computation.3 | async-start | bytes 7340032 | tf_op jit(solution)/shard_map/all_to_all | solution.py:22
  287.9 45.0 %all-to-all-done.3 = bf16[32,8,7168]{2,1,0:T(8,128)(2,1)} async-done(((bf16[32,8,7168]{2,1,0:T(8,128)(2,1)}), bf16[32,8,7168]{2,1,0:T(8,128)(2,1)}, u32[]{:S(2)}, u32[]{:S(2)}) %all-to-all-start.3) | async-done | bytes 3670048 | tf_op jit(solution)/shard_map/all_to_all | solution.py:22
  332.9 2.8 fusion.10
  339.7 3.1 collective-permute-start.6
  344.0 3.4 collective-permute-start.8
  349.6 3.2 collective-permute-done.9
  355.8 2.4 collective-permute-done.10
  365.7 2.8 collective-permute-start.12
  368.4 3.6 collective-permute-done.12
  372.1 7.3 %collective-permute-start.13 = (f32[8,128]{1,0:T(8,128)S(1)}, f32[8,128]{1,0:T(8,128)S(1)}, u32[]{:S(2)}, u32[]{:S(2)}) collective-permute-start(f32[8,128]{1,0:T(8,128)S(1)} %add.218), channel_id=1, source_target_pairs={{0,1},{1,0},{2,3},{3,2},{4,5},{5,4},{6,7},{7,6},{8,9},{9,8},{10,11... | collective-permute-start | bytes 12296 | tf_op jit(solution)/shard_map/ppermute | solution.py:58
  383.5 3.1 collective-permute-done.15
  389.1 2.4 collective-permute-start.17
  (87 shorter events, 47.0 us)
Async XLA Ops:
  2.9 4.1 %collective-permute-start = (bf16[2,14464]{1,0:T(2,128)(2,1)S(1)}, bf16[2,14464]{1,0:T(2,128)(2,1)S(1)}, u32[]{:S(2)}, u32[]{:S(2)}) collective-permute-start(bf16[2,14464]{1,0:T(2,128)(2,1)S(1)} %concatenate.18), channel_id=1, source_target_pairs={{0,32},{32,0},{64,96},{96,64},{128,160},{160,128},{192,224},{224,1... | collective-permute-start | bytes 173576 | tf_op jit(solution)/shard_map/ppermute | solution.py:34
  7.2 5.3 %collective-permute-start.1 = (bf16[4,14464]{1,0:T(4,128)(2,1)S(1)}, bf16[4,14464]{1,0:T(4,128)(2,1)S(1)}, u32[]{:S(2)}, u32[]{:S(2)}) collective-permute-start(bf16[4,14464]{1,0:T(4,128)(2,1)S(1)} %pad_maximum_fusion.4), channel_id=1, source_target_pairs={{0,64},{32,96},{64,0},{96,32},{128,192},{160,224},{192,128},{224,1... | collective-permute-start | bytes 347144 | tf_op jit(solution)/shard_map/ppermute | solution.py:34
  12.8 11.4 %collective-permute-start.2 = (bf16[8,14464]{1,0:T(8,128)(2,1)S(1)}, bf16[8,14464]{1,0:T(8,128)(2,1)S(1)}, u32[]{:S(2)}, u32[]{:S(2)}) collective-permute-start(bf16[8,14464]{1,0:T(8,128)(2,1)S(1)} %pad_maximum_fusion.3), channel_id=1, source_target_pairs={{0,128},{32,160},{64,192},{96,224},{128,0},{160,32},{192,64},{224,... | collective-permute-start | bytes 694280 | tf_op jit(solution)/shard_map/ppermute | solution.py:34
  27.8 97.4 %copy-start.4 = (bf16[1,7168,256]{2,1,0:T(8,128)(2,1)S(1)}, bf16[1,7168,256]{2,1,0:T(8,128)(2,1)}, u32[]{:S(2)}) copy-start(bf16[1,7168,256]{2,1,0:T(8,128)(2,1)} %param.12) | copy-start | bytes 11010052
  127.3 2.1 copy-start
  132.5 50.0 %all-to-all-start.1 = ((bf16[32,8,7168]{2,1,0:T(8,128)(2,1)}), bf16[32,8,7168]{2,1,0:T(8,128)(2,1)}, u32[]{:S(2)}, u32[]{:S(2)}) async-start(bf16[32,8,7168]{2,1,0:T(8,128)(2,1)} %fusion.1), calls=%async_computation.1 | async-start | bytes 7340032 | tf_op jit(solution)/shard_map/all_to_all | solution.py:22
  218.7 57.2 %copy-start.1 = (bf16[1,256,7168]{2,1,0:T(8,128)(2,1)S(1)}, bf16[1,256,7168]{2,1,0:T(8,128)(2,1)}, u32[]{:S(2)}) copy-start(bf16[1,256,7168]{2,1,0:T(8,128)(2,1)} %param.13) | copy-start | bytes 11010052
  282.9 50.0 %all-to-all-start.3 = ((bf16[32,8,7168]{2,1,0:T(8,128)(2,1)}), bf16[32,8,7168]{2,1,0:T(8,128)(2,1)}, u32[]{:S(2)}, u32[]{:S(2)}) async-start(bf16[32,8,7168]{2,1,0:T(8,128)(2,1)} %fusion.3), calls=%async_computation.3 | async-start | bytes 7340032 | tf_op jit(solution)/shard_map/all_to_all | solution.py:22
  287.9 64.9 %copy-start.6 = (bf16[1,2,7168]{2,1,0:T(2,128)(2,1)S(1)}, bf16[1,2,7168]{2,1,0:T(2,128)(2,1)}, u32[]{:S(2)}) copy-start(bf16[1,2,7168]{2,1,0:T(2,128)(2,1)} %param.8) | copy-start | bytes 86020
  336.1 7.9 %collective-permute-start.3 = (f32[2,7168]{1,0:T(2,128)S(1)}, f32[2,7168]{1,0:T(2,128)S(1)}, u32[]{:S(2)}, u32[]{:S(2)}) collective-permute-start(f32[2,7168]{1,0:T(2,128)S(1)} %get-tuple-element.8), channel_id=1, source_target_pairs={{0,32},{32,64},{64,96},{96,128},{128,160},{160,192},{192,224},{224... | collective-permute-start | bytes 172040 | tf_op jit(solution)/shard_map/ppermute | solution.py:26
  336.2 11.2 %collective-permute-start.4 = (f32[2,7168]{1,0:T(2,128)S(1)}, f32[2,7168]{1,0:T(2,128)S(1)}, u32[]{:S(2)}, u32[]{:S(2)}) collective-permute-start(f32[2,7168]{1,0:T(2,128)S(1)} %get-tuple-element.14), channel_id=1, source_target_pairs={{0,64},{32,96},{64,128},{96,160},{128,192},{160,224},{192,0},{224,... | collective-permute-start | bytes 172040 | tf_op jit(solution)/shard_map/ppermute | solution.py:26
  337.4 11.4 %collective-permute-start.5 = (f32[2,7168]{1,0:T(2,128)S(1)}, f32[2,7168]{1,0:T(2,128)S(1)}, u32[]{:S(2)}, u32[]{:S(2)}) collective-permute-start(f32[2,7168]{1,0:T(2,128)S(1)} %get-tuple-element.13), channel_id=1, source_target_pairs={{0,96},{32,128},{64,160},{96,192},{128,224},{160,0},{192,32},{224,... | collective-permute-start | bytes 172040 | tf_op jit(solution)/shard_map/ppermute | solution.py:26
  339.7 9.1 %collective-permute-start.6 = (f32[2,7168]{1,0:T(2,128)S(1)}, f32[2,7168]{1,0:T(2,128)S(1)}, u32[]{:S(2)}, u32[]{:S(2)}) collective-permute-start(f32[2,7168]{1,0:T(2,128)S(1)} %get-tuple-element.12), channel_id=1, source_target_pairs={{0,128},{32,160},{64,192},{96,224},{128,0},{160,32},{192,64},{224,... | collective-permute-start | bytes 172040 | tf_op jit(solution)/shard_map/ppermute | solution.py:26
  342.7 6.0 %collective-permute-start.7 = (f32[2,7168]{1,0:T(2,128)S(1)}, f32[2,7168]{1,0:T(2,128)S(1)}, u32[]{:S(2)}, u32[]{:S(2)}) collective-permute-start(f32[2,7168]{1,0:T(2,128)S(1)} %get-tuple-element.11), channel_id=1, source_target_pairs={{0,160},{32,192},{64,224},{96,0},{128,32},{160,64},{192,96},{224,1... | collective-permute-start | bytes 172040 | tf_op jit(solution)/shard_map/ppermute | solution.py:26
  344.0 5.6 %collective-permute-start.8 = (f32[2,7168]{1,0:T(2,128)S(1)}, f32[2,7168]{1,0:T(2,128)S(1)}, u32[]{:S(2)}, u32[]{:S(2)}) collective-permute-start(f32[2,7168]{1,0:T(2,128)S(1)} %get-tuple-element.10), channel_id=1, source_target_pairs={{0,192},{32,224},{64,0},{96,32},{128,64},{160,96},{192,128},{224,1... | collective-permute-start | bytes 172040 | tf_op jit(solution)/shard_map/ppermute | solution.py:26
  347.3 5.4 %collective-permute-start.9 = (f32[2,7168]{1,0:T(2,128)S(1)}, f32[2,7168]{1,0:T(2,128)S(1)}, u32[]{:S(2)}, u32[]{:S(2)}) collective-permute-start(f32[2,7168]{1,0:T(2,128)S(1)} %get-tuple-element.9), channel_id=1, source_target_pairs={{0,224},{32,0},{64,32},{96,64},{128,96},{160,128},{192,160},{224,1... | collective-permute-start | bytes 172040 | tf_op jit(solution)/shard_map/ppermute | solution.py:26
  355.6 2.7 collective-permute-start.10
  360.3 3.4 collective-permute-start.11
  365.7 6.4 %collective-permute-start.12 = (f32[8,128]{1,0:T(8,128)S(1)}, f32[8,128]{1,0:T(8,128)S(1)}, u32[]{:S(2)}, u32[]{:S(2)}) collective-permute-start(f32[8,128]{1,0:T(8,128)S(1)} %fusion.71), channel_id=1, source_target_pairs={{0,128},{32,160},{64,192},{96,224},{128,0},{160,32},{192,64},{224,... | collective-permute-start | bytes 12296 | tf_op jit(solution)/shard_map/ppermute | solution.py:58
  372.1 8.1 %collective-permute-start.13 = (f32[8,128]{1,0:T(8,128)S(1)}, f32[8,128]{1,0:T(8,128)S(1)}, u32[]{:S(2)}, u32[]{:S(2)}) collective-permute-start(f32[8,128]{1,0:T(8,128)S(1)} %add.218), channel_id=1, source_target_pairs={{0,1},{1,0},{2,3},{3,2},{4,5},{5,4},{6,7},{7,6},{8,9},{9,8},{10,11... | collective-permute-start | bytes 12296 | tf_op jit(solution)/shard_map/ppermute | solution.py:58
  380.2 2.5 collective-permute-start.14
  382.7 4.0 collective-permute-start.15
  386.6 2.5 collective-permute-start.16
  389.1 4.0 collective-permute-start.17
  (3 other events, 6.2 us)

commit v5 on v4

--- a/solution.py
+++ b/solution.py
@@ -29,15 +29,10 @@
 def gather_rows(value, axis):
     size = lax.axis_size(axis)
     me = lax.axis_index(axis)
-    step = 1
-    while step < size:
-        other = lax.ppermute(value, axis, [(i, i ^ step) for i in range(size)])
-        upper = (me // step) % 2 == 1
-        value = jnp.concatenate(
-            [jnp.where(upper, other, value), jnp.where(upper, value, other)], axis=0
-        )
-        step *= 2
-    return value
+    got = jnp.stack([value] + [shifted(value, axis, size, s) for s in range(1, size)])
+    source_slot = (me - jnp.arange(size)) % size
+    order = jnp.zeros((size,), jnp.int32).at[source_slot].set(jnp.arange(size))
+    return got[order].reshape(size * value.shape[0], *value.shape[1:])
 
 
 def scatter_sum_rows(value, axis):
@@ -180,7 +175,7 @@
             jnp.where(row & (lane == 2), jnp.sum(probe_f * probe_f), 0.0),
         ),
     ).astype(F32)
-    sums = butterfly_sum(butterfly_sum(sums, "dp"), "expert")
+    sums = butterfly_sum(butterfly_sum(lax.optimization_barrier(sums), "dp"), "expert")
     probe_result, result_sq, probe_sq = sums[0, 0], sums[0, 1], sums[0, 2]
     total_cells = lax.axis_size("dp") * lax.axis_size("expert") * tok_dev * model_width
     next_tangent = (result * lax.rsqrt(result_sq / total_cells + 1e-06)).astype(BF16)

time: 401 us -> 394 us (0.983)
  blocking collectives: 187 us -> 179 us
  other arithmetic: 10.7 us -> 6 us
    ppermute x7 -> x14, starting transfers between devices: 12.6 us -> 27.9 us  [shifted(): lax.ppermute(value, axis, [(i, (i + step) % size) for i in range(size)])]
    ppermute x3 -> x0, starting transfers between devices: 13.5 us -> none  [gather_rows(): other = lax.ppermute(value, axis, [(i, i ^ step) for i in range(size)])]
    ppermute x3 -> x0, waiting for transfers between devices: 7.31 us -> none  [gather_rows(): other = lax.ppermute(value, axis, [(i, i ^ step) for i in range(size)])]
    ppermute x7 -> x14, waiting for transfers between devices: 4.03 us -> 8.92 us  [shifted(): lax.ppermute(value, axis, [(i, (i + step) % size) for i in range(size)])]
    all_to_all x2, blocking collectives: 155 us -> 150 us  [exchange(): lax.all_to_all(value, 'expert', split_axis=0, concat_axis=0, tiled=True)]
  transfers between devices with their start and end apart: 20 -> 24, of which waited for: 15 -> 13; matrix products, arithmetic and copies ran while one was open for 0% -> 0% of each run, Pallas kernels for 0% -> 0%
where the time goes in v5:
time: 394 us; the launch traced here: 390 us
  blocking collectives  179 us (45%)
  waiting for transfers between devices  118 us (30%)
  starting transfers between devices  55.4 us (14%)
  matrix products  21.3 us (5%)
  local copies, waits for them, and re-layouts  6.73 us (2%)
  other arithmetic  6 us (2%)
  between operations  4.28 us (1%)
    all_to_all x2, blocking collectives, exchange(): lax.all_to_all(value, 'expert', split_axis=0, concat_axis=0, tiled=True)  150 us
    all_to_all x2, waiting for transfers between devices, exchange(): lax.all_to_all(value, 'expert', split_axis=0, concat_axis=0, tiled=True)  89.9 us
    psum x1, blocking collectives, body(): product_bf = lax.psum(product_part, 'dp').astype(BF16)  28.3 us
    ppermute x14, starting transfers between devices, shifted(): lax.ppermute(value, axis, [(i, (i + step) % size) for i in range(size)])  27.9 us
    ppermute x8, waiting for transfers between devices, butterfly_sum(): lax.ppermute(value, axis, [(i, i ^ step) for i in range(size)])  18.7 us
    ppermute x8, starting transfers between devices, butterfly_sum(): lax.ppermute(value, axis, [(i, i ^ step) for i in range(size)])  17.8 us
    all_to_all x2, starting transfers between devices, exchange(): lax.all_to_all(value, 'expert', split_axis=0, concat_axis=0, tiled=True)  9.67 us
    ppermute x14, waiting for transfers between devices, shifted(): lax.ppermute(value, axis, [(i, (i + step) % size) for i in range(size)])  8.92 us
  transfers between devices with their start and end apart: 24, of which 13 were waited for; matrix products, arithmetic and copies ran while one was open for 0% of the time, Pallas kernels for 0%

profile of v5, /device:TPU:1, one launch (start us, length us, event | category | flops | bytes accessed | tf_op | source)
XLA Modules:
  0.0 389.9 jit_solution(15773377590094714650)
XLA Ops:
  2.9 2.5 collective-permute-start
  5.4 3.0 collective-permute-start.1
  8.4 3.8 collective-permute-start.2
  12.6 4.5 %collective-permute-start.4 = (bf16[2,14464]{1,0:T(2,128)(2,1)S(1)}, bf16[2,14464]{1,0:T(2,128)(2,1)S(1)}, u32[]{:S(2)}, u32[]{:S(2)}) collective-permute-start(bf16[2,14464]{1,0:T(2,128)(2,1)S(1)} %concatenate.9), channel_id=1, source_target_pairs={{0,160},{32,192},{64,224},{96,0},{128,32},{160,64},{192,96},{224,1... | collective-permute-start | bytes 173576 | tf_op jit(solution)/shard_map/ppermute | solution.py:26
  17.8 2.5 collective-permute-start.5
  21.4 5.1 %collective-permute-done.5 = bf16[2,14464]{1,0:T(2,128)(2,1)S(1)} collective-permute-done((bf16[2,14464]{1,0:T(2,128)(2,1)S(1)}, bf16[2,14464]{1,0:T(2,128)(2,1)S(1)}, u32[]{:S(2)}, u32[]{:S(2)}) %collective-permute-start.5) | collective-permute-done | bytes 57888 | tf_op jit(solution)/shard_map/ppermute | solution.py:26
  31.7 93.0 %all_to_all.20 = bf16[32,16,7168]{2,1,0:T(8,128)(2,1)S(1)} all-to-all(bf16[32,16,7168]{2,1,0:T(8,128)(2,1)S(1)} %bitcast.168), channel_id=1, replica_groups=mesh['dp'=8,'expert'=32] {'expert'}, dimensions={0} | all-to-all | bytes 14680064 | tf_op jit(solution)/shard_map/all_to_all | solution.py:22
  128.8 3.1 fusion.1
  131.9 4.8 %all-to-all-start.1 = ((bf16[32,8,7168]{2,1,0:T(8,128)(2,1)}), bf16[32,8,7168]{2,1,0:T(8,128)(2,1)}, u32[]{:S(2)}, u32[]{:S(2)}) async-start(bf16[32,8,7168]{2,1,0:T(8,128)(2,1)} %fusion.1), calls=%async_computation.1 | async-start | bytes 7340032 | tf_op jit(solution)/shard_map/all_to_all | solution.py:22
  137.0 44.9 %all-to-all-done.1 = bf16[32,8,7168]{2,1,0:T(8,128)(2,1)} async-done(((bf16[32,8,7168]{2,1,0:T(8,128)(2,1)}), bf16[32,8,7168]{2,1,0:T(8,128)(2,1)}, u32[]{:S(2)}, u32[]{:S(2)}) %all-to-all-start.1) | async-done | bytes 3670048 | tf_op jit(solution)/shard_map/all_to_all | solution.py:22
  181.9 2.8 fusion.14
  184.7 28.3 %all-reduce.1 = bf16[16,7168]{1,0:T(8,128)(2,1)S(1)} all-reduce(f32[16,7168]{1,0:T(8,128)S(1)} %slice_add_fusion.1), channel_id=1, replica_groups=mesh['dp'=8,'expert'=32] {'dp'}, use_global_device_ids=true, to_apply=%region_5.6 | all-reduce | flops 114688 | bytes 688128 | tf_op jit(solution)/shard_map/psum | solution.py:150
  214.2 57.5 %all_to_all.21 = bf16[32,8,7168]{2,1,0:T(8,128)(2,1)S(1)} all-to-all(bf16[32,8,7168]{2,1,0:T(8,128)(2,1)S(1)} %fusion.2), channel_id=1, replica_groups=mesh['dp'=8,'expert'=32] {'expert'}, dimensions={0} | all-to-all | bytes 7340032 | tf_op jit(solution)/shard_map/all_to_all | solution.py:22
  275.7 3.0 fusion.3
  278.7 4.8 %all-to-all-start.3 = ((bf16[32,8,7168]{2,1,0:T(8,128)(2,1)}), bf16[32,8,7168]{2,1,0:T(8,128)(2,1)}, u32[]{:S(2)}, u32[]{:S(2)}) async-start(bf16[32,8,7168]{2,1,0:T(8,128)(2,1)} %fusion.3), calls=%async_computation.3 | async-start | bytes 7340032 | tf_op jit(solution)/shard_map/all_to_all | solution.py:22
  283.7 45.0 %all-to-all-done.3 = bf16[32,8,7168]{2,1,0:T(8,128)(2,1)} async-done(((bf16[32,8,7168]{2,1,0:T(8,128)(2,1)}), bf16[32,8,7168]{2,1,0:T(8,128)(2,1)}, u32[]{:S(2)}, u32[]{:S(2)}) %all-to-all-start.3) | async-done | bytes 3670048 | tf_op jit(solution)/shard_map/all_to_all | solution.py:22
  328.7 2.8 fusion.10
  348.9 3.0 collective-permute-start.14
  353.0 3.1 collective-permute-start.15
  357.1 2.5 collective-permute-start.16
  359.5 3.9 %collective-permute-done.16 = f32[8,128]{1,0:T(8,128)S(1)} collective-permute-done((f32[8,128]{1,0:T(8,128)S(1)}, f32[8,128]{1,0:T(8,128)S(1)}, u32[]{:S(2)}, u32[]{:S(2)}) %collective-permute-start.16) | collective-permute-done | bytes 4128 | tf_op jit(solution)/shard_map/ppermute | solution.py:53
  363.4 8.4 %collective-permute-start.17 = (f32[8,128]{1,0:T(8,128)S(1)}, f32[8,128]{1,0:T(8,128)S(1)}, u32[]{:S(2)}, u32[]{:S(2)}) collective-permute-start(f32[8,128]{1,0:T(8,128)S(1)} %add.232), channel_id=1, source_target_pairs={{0,1},{1,0},{2,3},{3,2},{4,5},{5,4},{6,7},{7,6},{8,9},{9,8},{10,11... | collective-permute-start | bytes 12296 | tf_op jit(solution)/shard_map/ppermute | solution.py:53
  375.1 4.0 %collective-permute-done.19 = f32[8,128]{1,0:T(8,128)S(1)} collective-permute-done((f32[8,128]{1,0:T(8,128)S(1)}, f32[8,128]{1,0:T(8,128)S(1)}, u32[]{:S(2)}, u32[]{:S(2)}) %collective-permute-start.19) | collective-permute-done | bytes 4128 | tf_op jit(solution)/shard_map/ppermute | solution.py:53
  382.4 3.1 collective-permute-done.21
  (106 shorter events, 46.5 us)
Async XLA Ops:
  2.9 14.9 %collective-permute-start = (bf16[2,14464]{1,0:T(2,128)(2,1)S(1)}, bf16[2,14464]{1,0:T(2,128)(2,1)S(1)}, u32[]{:S(2)}, u32[]{:S(2)}) collective-permute-start(bf16[2,14464]{1,0:T(2,128)(2,1)S(1)} %concatenate.9), channel_id=1, source_target_pairs={{0,32},{32,64},{64,96},{96,128},{128,160},{160,192},{192,224},{224... | collective-permute-start | bytes 173576 | tf_op jit(solution)/shard_map/ppermute | solution.py:26
  5.4 14.9 %collective-permute-start.1 = (bf16[2,14464]{1,0:T(2,128)(2,1)S(1)}, bf16[2,14464]{1,0:T(2,128)(2,1)S(1)}, u32[]{:S(2)}, u32[]{:S(2)}) collective-permute-start(bf16[2,14464]{1,0:T(2,128)(2,1)S(1)} %concatenate.9), channel_id=1, source_target_pairs={{0,64},{32,96},{64,128},{96,160},{128,192},{160,224},{192,0},{224,... | collective-permute-start | bytes 173576 | tf_op jit(solution)/shard_map/ppermute | solution.py:26
  8.4 12.8 %collective-permute-start.2 = (bf16[2,14464]{1,0:T(2,128)(2,1)S(1)}, bf16[2,14464]{1,0:T(2,128)(2,1)S(1)}, u32[]{:S(2)}, u32[]{:S(2)}) collective-permute-start(bf16[2,14464]{1,0:T(2,128)(2,1)S(1)} %concatenate.9), channel_id=1, source_target_pairs={{0,96},{32,128},{64,160},{96,192},{128,224},{160,0},{192,32},{224,... | collective-permute-start | bytes 173576 | tf_op jit(solution)/shard_map/ppermute | solution.py:26
  12.2 9.1 %collective-permute-start.3 = (bf16[2,14464]{1,0:T(2,128)(2,1)S(1)}, bf16[2,14464]{1,0:T(2,128)(2,1)S(1)}, u32[]{:S(2)}, u32[]{:S(2)}) collective-permute-start(bf16[2,14464]{1,0:T(2,128)(2,1)S(1)} %concatenate.9), channel_id=1, source_target_pairs={{0,128},{32,160},{64,192},{96,224},{128,0},{160,32},{192,64},{224,... | collective-permute-start | bytes 173576 | tf_op jit(solution)/shard_map/ppermute | solution.py:26
  12.6 8.7 %collective-permute-start.4 = (bf16[2,14464]{1,0:T(2,128)(2,1)S(1)}, bf16[2,14464]{1,0:T(2,128)(2,1)S(1)}, u32[]{:S(2)}, u32[]{:S(2)}) collective-permute-start(bf16[2,14464]{1,0:T(2,128)(2,1)S(1)} %concatenate.9), channel_id=1, source_target_pairs={{0,160},{32,192},{64,224},{96,0},{128,32},{160,64},{192,96},{224,1... | collective-permute-start | bytes 173576 | tf_op jit(solution)/shard_map/ppermute | solution.py:26
  17.8 8.7 %collective-permute-start.5 = (bf16[2,14464]{1,0:T(2,128)(2,1)S(1)}, bf16[2,14464]{1,0:T(2,128)(2,1)S(1)}, u32[]{:S(2)}, u32[]{:S(2)}) collective-permute-start(bf16[2,14464]{1,0:T(2,128)(2,1)S(1)} %concatenate.9), channel_id=1, source_target_pairs={{0,192},{32,224},{64,0},{96,32},{128,64},{160,96},{192,128},{224,1... | collective-permute-start | bytes 173576 | tf_op jit(solution)/shard_map/ppermute | solution.py:26
  20.4 6.2 %collective-permute-start.6 = (bf16[2,14464]{1,0:T(2,128)(2,1)S(1)}, bf16[2,14464]{1,0:T(2,128)(2,1)S(1)}, u32[]{:S(2)}, u32[]{:S(2)}) collective-permute-start(bf16[2,14464]{1,0:T(2,128)(2,1)S(1)} %concatenate.9), channel_id=1, source_target_pairs={{0,224},{32,0},{64,32},{96,64},{128,96},{160,128},{192,160},{224,1... | collective-permute-start | bytes 173576 | tf_op jit(solution)/shard_map/ppermute | solution.py:26
  131.9 50.0 %all-to-all-start.1 = ((bf16[32,8,7168]{2,1,0:T(8,128)(2,1)}), bf16[32,8,7168]{2,1,0:T(8,128)(2,1)}, u32[]{:S(2)}, u32[]{:S(2)}) async-start(bf16[32,8,7168]{2,1,0:T(8,128)(2,1)} %fusion.1), calls=%async_computation.1 | async-start | bytes 7340032 | tf_op jit(solution)/shard_map/all_to_all | solution.py:22
  278.7 50.0 %all-to-all-start.3 = ((bf16[32,8,7168]{2,1,0:T(8,128)(2,1)}), bf16[32,8,7168]{2,1,0:T(8,128)(2,1)}, u32[]{:S(2)}, u32[]{:S(2)}) async-start(bf16[32,8,7168]{2,1,0:T(8,128)(2,1)} %fusion.3), calls=%async_computation.3 | async-start | bytes 7340032 | tf_op jit(solution)/shard_map/all_to_all | solution.py:22
  331.9 7.1 %collective-permute-start.10 = (f32[2,7168]{1,0:T(2,128)S(1)}, f32[2,7168]{1,0:T(2,128)S(1)}, u32[]{:S(2)}, u32[]{:S(2)}) collective-permute-start(f32[2,7168]{1,0:T(2,128)S(1)} %get-tuple-element.12), channel_id=1, source_target_pairs={{0,128},{32,160},{64,192},{96,224},{128,0},{160,32},{192,64},{224,... | collective-permute-start | bytes 172040 | tf_op jit(solution)/shard_map/ppermute | solution.py:26
  334.0 6.0 %collective-permute-start.11 = (f32[2,7168]{1,0:T(2,128)S(1)}, f32[2,7168]{1,0:T(2,128)S(1)}, u32[]{:S(2)}, u32[]{:S(2)}) collective-permute-start(f32[2,7168]{1,0:T(2,128)S(1)} %get-tuple-element.11), channel_id=1, source_target_pairs={{0,160},{32,192},{64,224},{96,0},{128,32},{160,64},{192,96},{224,1... | collective-permute-start | bytes 172040 | tf_op jit(solution)/shard_map/ppermute | solution.py:26
  335.1 7.2 %collective-permute-start.12 = (f32[2,7168]{1,0:T(2,128)S(1)}, f32[2,7168]{1,0:T(2,128)S(1)}, u32[]{:S(2)}, u32[]{:S(2)}) collective-permute-start(f32[2,7168]{1,0:T(2,128)S(1)} %get-tuple-element.10), channel_id=1, source_target_pairs={{0,192},{32,224},{64,0},{96,32},{128,64},{160,96},{192,128},{224,1... | collective-permute-start | bytes 172040 | tf_op jit(solution)/shard_map/ppermute | solution.py:26
  337.5 7.1 %collective-permute-start.13 = (f32[2,7168]{1,0:T(2,128)S(1)}, f32[2,7168]{1,0:T(2,128)S(1)}, u32[]{:S(2)}, u32[]{:S(2)}) collective-permute-start(f32[2,7168]{1,0:T(2,128)S(1)} %get-tuple-element.9), channel_id=1, source_target_pairs={{0,224},{32,0},{64,32},{96,64},{128,96},{160,128},{192,160},{224,1... | collective-permute-start | bytes 172040 | tf_op jit(solution)/shard_map/ppermute | solution.py:26
  338.8 5.9 %collective-permute-start.7 = (f32[2,7168]{1,0:T(2,128)S(1)}, f32[2,7168]{1,0:T(2,128)S(1)}, u32[]{:S(2)}, u32[]{:S(2)}) collective-permute-start(f32[2,7168]{1,0:T(2,128)S(1)} %get-tuple-element.8), channel_id=1, source_target_pairs={{0,32},{32,64},{64,96},{96,128},{128,160},{160,192},{192,224},{224... | collective-permute-start | bytes 172040 | tf_op jit(solution)/shard_map/ppermute | solution.py:26
  339.0 5.7 %collective-permute-start.8 = (f32[2,7168]{1,0:T(2,128)S(1)}, f32[2,7168]{1,0:T(2,128)S(1)}, u32[]{:S(2)}, u32[]{:S(2)}) collective-permute-start(f32[2,7168]{1,0:T(2,128)S(1)} %get-tuple-element.14), channel_id=1, source_target_pairs={{0,64},{32,96},{64,128},{96,160},{128,192},{160,224},{192,0},{224,... | collective-permute-start | bytes 172040 | tf_op jit(solution)/shard_map/ppermute | solution.py:26
  340.0 6.1 %collective-permute-start.9 = (f32[2,7168]{1,0:T(2,128)S(1)}, f32[2,7168]{1,0:T(2,128)S(1)}, u32[]{:S(2)}, u32[]{:S(2)}) collective-permute-start(f32[2,7168]{1,0:T(2,128)S(1)} %get-tuple-element.13), channel_id=1, source_target_pairs={{0,96},{32,128},{64,160},{96,192},{128,224},{160,0},{192,32},{224,... | collective-permute-start | bytes 172040 | tf_op jit(solution)/shard_map/ppermute | solution.py:26
  348.9 4.0 %collective-permute-start.14 = (f32[8,128]{1,0:T(8,128)S(1)}, f32[8,128]{1,0:T(8,128)S(1)}, u32[]{:S(2)}, u32[]{:S(2)}) collective-permute-start(f32[8,128]{1,0:T(8,128)S(1)} %select_select_fusion), channel_id=1, source_target_pairs={{0,32},{32,0},{64,96},{96,64},{128,160},{160,128},{192,224},{224,1... | collective-permute-start | bytes 12296 | tf_op jit(solution)/shard_map/ppermute | solution.py:53
  353.0 4.1 %collective-permute-start.15 = (f32[8,128]{1,0:T(8,128)S(1)}, f32[8,128]{1,0:T(8,128)S(1)}, u32[]{:S(2)}, u32[]{:S(2)}) collective-permute-start(f32[8,128]{1,0:T(8,128)S(1)} %add.230), channel_id=1, source_target_pairs={{0,64},{32,96},{64,0},{96,32},{128,192},{160,224},{192,128},{224,1... | collective-permute-start | bytes 12296 | tf_op jit(solution)/shard_map/ppermute | solution.py:53
  357.1 6.4 %collective-permute-start.16 = (f32[8,128]{1,0:T(8,128)S(1)}, f32[8,128]{1,0:T(8,128)S(1)}, u32[]{:S(2)}, u32[]{:S(2)}) collective-permute-start(f32[8,128]{1,0:T(8,128)S(1)} %add.231), channel_id=1, source_target_pairs={{0,128},{32,160},{64,192},{96,224},{128,0},{160,32},{192,64},{224,... | collective-permute-start | bytes 12296 | tf_op jit(solution)/shard_map/ppermute | solution.py:53
  363.4 9.2 %collective-permute-start.17 = (f32[8,128]{1,0:T(8,128)S(1)}, f32[8,128]{1,0:T(8,128)S(1)}, u32[]{:S(2)}, u32[]{:S(2)}) collective-permute-start(f32[8,128]{1,0:T(8,128)S(1)} %add.232), channel_id=1, source_target_pairs={{0,1},{1,0},{2,3},{3,2},{4,5},{5,4},{6,7},{7,6},{8,9},{9,8},{10,11... | collective-permute-start | bytes 12296 | tf_op jit(solution)/shard_map/ppermute | solution.py:53
  372.7 2.5 collective-permute-start.18
  375.1 4.0 %collective-permute-start.19 = (f32[8,128]{1,0:T(8,128)S(1)}, f32[8,128]{1,0:T(8,128)S(1)}, u32[]{:S(2)}, u32[]{:S(2)}) collective-permute-start(f32[8,128]{1,0:T(8,128)S(1)} %add.234), channel_id=1, source_target_pairs={{0,4},{1,5},{2,6},{3,7},{4,0},{5,1},{6,2},{7,3},{8,12},{9,13},{10,... | collective-permute-start | bytes 12296 | tf_op jit(solution)/shard_map/ppermute | solution.py:53
  379.1 2.5 collective-permute-start.20
  381.5 4.0 %collective-permute-start.21 = (f32[8,128]{1,0:T(8,128)S(1)}, f32[8,128]{1,0:T(8,128)S(1)}, u32[]{:S(2)}, u32[]{:S(2)}) collective-permute-start(f32[8,128]{1,0:T(8,128)S(1)} %add.236), channel_id=1, source_target_pairs={{0,16},{1,17},{2,18},{3,19},{4,20},{5,21},{6,22},{7,23},{8,24},{9,... | collective-permute-start | bytes 12296 | tf_op jit(solution)/shard_map/ppermute | solution.py:53
  (7 other events, 221.1 us)

commit v6 on v5

--- a/solution.py
+++ b/solution.py
@@ -28,22 +28,21 @@
 
 def gather_rows(value, axis):
     size = lax.axis_size(axis)
-    me = lax.axis_index(axis)
-    got = jnp.stack([value] + [shifted(value, axis, size, s) for s in range(1, size)])
-    source_slot = (me - jnp.arange(size)) % size
-    order = jnp.zeros((size,), jnp.int32).at[source_slot].set(jnp.arange(size))
-    return got[order].reshape(size * value.shape[0], *value.shape[1:])
+    copies = jnp.broadcast_to(value[None], (size,) + value.shape).reshape(
+        size * value.shape[0], *value.shape[1:]
+    )
+    return lax.all_to_all(copies, axis, split_axis=0, concat_axis=0, tiled=True)
 
 
 def scatter_sum_rows(value, axis):
     size = lax.axis_size(axis)
-    me = lax.axis_index(axis)
-    blocks = value.reshape(size, value.shape[0] // size, *value.shape[1:])
-    total = lax.dynamic_index_in_dim(blocks, me, 0, keepdims=False)
-    for s in range(1, size):
-        outgoing = lax.dynamic_index_in_dim(blocks, (me + s) % size, 0, keepdims=False)
-        total = total + shifted(outgoing, axis, size, s)
-    return total
+    got = lax.all_to_all(value, axis, split_axis=0, concat_axis=0, tiled=True)
+    return jnp.sum(got.reshape(size, value.shape[0] // size, *value.shape[1:]), axis=0)
+
+
+def total_sum(value, axis):
+    size = lax.axis_size(axis)
+    return jnp.sum(gather_rows(value, axis).reshape(size, *value.shape), axis=0)
 
 
 def butterfly_sum(value, axis):
@@ -165,17 +164,16 @@
     result = scatter_sum_rows(result_part, "dp")
     probe_f = tangent[0].astype(F32)
     lane = jnp.arange(128)[None, :]
-    row = jnp.arange(8)[:, None] == 0
     sums = jnp.where(
-        row & (lane == 0),
+        lane == 0,
         jnp.sum(probe_f * result),
         jnp.where(
-            row & (lane == 1),
+            lane == 1,
             jnp.sum(result * result),
-            jnp.where(row & (lane == 2), jnp.sum(probe_f * probe_f), 0.0),
+            jnp.where(lane == 2, jnp.sum(probe_f * probe_f), 0.0),
         ),
     ).astype(F32)
-    sums = butterfly_sum(butterfly_sum(lax.optimization_barrier(sums), "dp"), "expert")
+    sums = total_sum(total_sum(lax.optimization_barrier(sums), "dp"), "expert")
     probe_result, result_sq, probe_sq = sums[0, 0], sums[0, 1], sums[0, 2]
     total_cells = lax.axis_size("dp") * lax.axis_size("expert") * tok_dev * model_width
     next_tangent = (result * lax.rsqrt(result_sq / total_cells + 1e-06)).astype(BF16)

time: 394 us -> 375 us (0.952)
  blocking collectives: 179 us -> 266 us
  waiting for transfers between devices: 118 us -> 61.5 us
  starting transfers between devices: 55.4 us -> 13.8 us
  matrix products: 21.3 us -> 17.3 us
    all_to_all x2 -> x3, blocking collectives: 150 us -> 199 us  [exchange(): lax.all_to_all(value, 'expert', split_axis=0, concat_axis=0, tiled=True)]
    ppermute x22 -> x0, starting transfers between devices: 45.8 us -> none  [the longest x14 27.9 us: shifted(): lax.ppermute(value, axis, [(i, (i + step) % size) for i in range(size)])]
    all_to_all x2 -> x1, waiting for transfers between devices: 89.9 us -> 44.9 us  [exchange(): lax.all_to_all(value, 'expert', split_axis=0, concat_axis=0, tiled=True)]
    all_to_all x0 -> x3, blocking collectives: none -> 40.4 us  [the longest x2 22.4 us: gather_rows(): return lax.all_to_all(copies, axis, split_axis=0, concat_axis=0, tiled=True)]
    ppermute x22 -> x0, waiting for transfers between devices: 27.6 us -> none  [the longest x8 18.7 us: butterfly_sum(): lax.ppermute(value, axis, [(i, i ^ step) for i in range(size)])]
    all_to_all x0 -> x1, waiting for transfers between devices: none -> 16.6 us  [gather_rows(): return lax.all_to_all(copies, axis, split_axis=0, concat_axis=0, tiled=True)]
    all_to_all x0 -> x1, starting transfers between devices: none -> 9 us  [gather_rows(): return lax.all_to_all(copies, axis, split_axis=0, concat_axis=0, tiled=True)]
    all_to_all x2 -> x1, starting transfers between devices: 9.67 us -> 4.8 us  [exchange(): lax.all_to_all(value, 'expert', split_axis=0, concat_axis=0, tiled=True)]
  transfers between devices with their start and end apart: 24 -> 2, of which waited for: 13 -> 2; matrix products, arithmetic and copies ran while one was open for 0% -> 0% of each run, Pallas kernels for 0% -> 0%
where the time goes in v6:
time: 375 us; the launch traced here: 374 us
  blocking collectives  266 us (71%)
  waiting for transfers between devices  61.5 us (16%)
  matrix products  17.3 us (5%)
  starting transfers between devices  13.8 us (4%)
  other arithmetic  6.11 us (2%)
  local copies, waits for them, and re-layouts  5.24 us (1%)
  between operations  4.13 us (1%)
    all_to_all x3, blocking collectives, exchange(): lax.all_to_all(value, 'expert', split_axis=0, concat_axis=0, tiled=True)  199 us
    all_to_all x1, waiting for transfers between devices, exchange(): lax.all_to_all(value, 'expert', split_axis=0, concat_axis=0, tiled=True)  44.9 us
    psum x1, blocking collectives, body(): product_bf = lax.psum(product_part, 'dp').astype(BF16)  26.1 us
    all_to_all x2, blocking collectives, gather_rows(): return lax.all_to_all(copies, axis, split_axis=0, concat_axis=0, tiled=True)  22.4 us
    all_to_all x1, blocking collectives, scatter_sum_rows(): got = lax.all_to_all(value, axis, split_axis=0, concat_axis=0, tiled=True)  18 us
    all_to_all x1, waiting for transfers between devices, gather_rows(): return lax.all_to_all(copies, axis, split_axis=0, concat_axis=0, tiled=True)  16.6 us
    all_to_all x1, starting transfers between devices, gather_rows(): return lax.all_to_all(copies, axis, split_axis=0, concat_axis=0, tiled=True)  9 us
  transfers between devices with their start and end apart: 2, of which 2 were waited for; matrix products, arithmetic and copies ran while one was open for 0% of the time, Pallas kernels for 0%

profile of v6, /device:TPU:1, one launch (start us, length us, event | category | flops | bytes accessed | tf_op | source)
XLA Modules:
  0.0 374.0 jit_solution(7607076914099491467)
XLA Ops:
  2.0 0.9 concatenate.9
  2.9 1.0 broadcast_in_dim.32
  3.9 9.0 %all-to-all-start = ((bf16[8,2,14464]{2,1,0:T(2,128)(2,1)}), bf16[8,2,14464]{2,1,0:T(2,128)(2,1)S(1)}, u32[]{:S(2)}, u32[]{:S(2)}) async-start(bf16[8,2,14464]{2,1,0:T(2,128)(2,1)} %broadcast_in_dim.32), calls=%async_computation | async-start | bytes 925696 | tf_op jit(solution)/shard_map/all_to_all | solution.py:34
  12.9 16.6 %all-to-all-done = bf16[8,2,14464]{2,1,0:T(2,128)(2,1)S(1)} async-done(((bf16[8,2,14464]{2,1,0:T(2,128)(2,1)}), bf16[8,2,14464]{2,1,0:T(2,128)(2,1)S(1)}, u32[]{:S(2)}, u32[]{:S(2)}) %all-to-all-start) | async-done | bytes 462880 | tf_op jit(solution)/shard_map/all_to_all | solution.py:34
  31.0 2.0 convolution_convert_fusion
  33.1 92.2 %all_to_all.50 = bf16[32,16,7168]{2,1,0:T(8,128)(2,1)S(1)} all-to-all(bf16[32,16,7168]{2,1,0:T(8,128)(2,1)S(1)} %bitcast.125), channel_id=1, replica_groups=mesh['dp'=8,'expert'=32] {'expert'}, dimensions={0} | all-to-all | bytes 14680064 | tf_op jit(solution)/shard_map/all_to_all | solution.py:22
  125.2 2.1 fusion.6
  127.3 2.1 fusion.4
  129.4 3.1 fusion.1
  132.5 4.8 %all-to-all-start.2 = ((bf16[32,8,7168]{2,1,0:T(8,128)(2,1)}), bf16[32,8,7168]{2,1,0:T(8,128)(2,1)}, u32[]{:S(2)}, u32[]{:S(2)}) async-start(bf16[32,8,7168]{2,1,0:T(8,128)(2,1)} %fusion.1), calls=%async_computation.2 | async-start | bytes 7340032 | tf_op jit(solution)/shard_map/all_to_all | solution.py:22
  137.5 44.9 %all-to-all-done.2 = bf16[32,8,7168]{2,1,0:T(8,128)(2,1)} async-done(((bf16[32,8,7168]{2,1,0:T(8,128)(2,1)}), bf16[32,8,7168]{2,1,0:T(8,128)(2,1)}, u32[]{:S(2)}, u32[]{:S(2)}) %all-to-all-start.2) | async-done | bytes 3670048 | tf_op jit(solution)/shard_map/all_to_all | solution.py:22
  182.4 2.8 fusion.14
  185.3 26.1 %all-reduce.1 = bf16[16,7168]{1,0:T(8,128)(2,1)S(1)} all-reduce(f32[16,7168]{1,0:T(8,128)S(1)} %slice_add_fusion.1), channel_id=1, replica_groups=mesh['dp'=8,'expert'=32] {'dp'}, use_global_device_ids=true, to_apply=%region_4.5 | all-reduce | flops 114688 | bytes 688128 | tf_op jit(solution)/shard_map/psum | solution.py:149
  211.3 1.1 fusion.2
  212.5 58.5 %all_to_all.51 = bf16[32,8,7168]{2,1,0:T(8,128)(2,1)S(1)} all-to-all(bf16[32,8,7168]{2,1,0:T(8,128)(2,1)S(1)} %fusion.2), channel_id=1, replica_groups=mesh['dp'=8,'expert'=32] {'expert'}, dimensions={0} | all-to-all | bytes 7340032 | tf_op jit(solution)/shard_map/all_to_all | solution.py:22
  271.0 1.1 fusion.12
  272.1 0.9 copy-done.3
  273.0 1.2 fusion.19
  275.0 1.2 fusion.3
  276.2 48.8 %all_to_all.52 = bf16[32,8,7168]{2,1,0:T(8,128)(2,1)S(1)} all-to-all(bf16[32,8,7168]{2,1,0:T(8,128)(2,1)S(1)} %fusion.3), channel_id=1, replica_groups=mesh['dp'=8,'expert'=32] {'expert'}, dimensions={0} | all-to-all | bytes 7340032 | tf_op jit(solution)/shard_map/all_to_all | solution.py:22
  326.1 18.0 %all_to_all.53 = f32[8,2,7168]{2,1,0:T(2,128)S(1)} all-to-all(f32[8,2,7168]{2,1,0:T(2,128)S(1)} %all_to_all.38), channel_id=1, replica_groups=mesh['dp'=8,'expert'=32] {'dp'}, dimensions={0} | all-to-all | bytes 917504 | tf_op jit(solution)/shard_map/all_to_all | solution.py:39
  345.1 2.0 compare_select_fusion.2
  347.1 8.9 %all_to_all.54 = f32[8,1,128]{2,1,0:T(1,128)S(1)} all-to-all(f32[8,1,128]{2,1,0:T(1,128)S(1)} %reshape.189), channel_id=1, replica_groups=mesh['dp'=8,'expert'=32] {'dp'}, dimensions={0} | all-to-all | bytes 8192 | tf_op jit(solution)/shard_map/all_to_all | solution.py:34
  356.0 13.4 %all_to_all.55 = f32[32,1,128]{2,1,0:T(1,128)S(1)} all-to-all(f32[32,1,128]{2,1,0:T(1,128)S(1)} %reshape.190), channel_id=1, replica_groups=mesh['dp'=8,'expert'=32] {'expert'}, dimensions={0} | all-to-all | bytes 32768 | tf_op jit(solution)/shard_map/all_to_all | solution.py:34
  (46 shorter events, 7.3 us)
Async XLA Ops:
  3.9 25.6 %all-to-all-start = ((bf16[8,2,14464]{2,1,0:T(2,128)(2,1)}), bf16[8,2,14464]{2,1,0:T(2,128)(2,1)S(1)}, u32[]{:S(2)}, u32[]{:S(2)}) async-start(bf16[8,2,14464]{2,1,0:T(2,128)(2,1)} %broadcast_in_dim.32), calls=%async_computation | async-start | bytes 925696 | tf_op jit(solution)/shard_map/all_to_all | solution.py:34
  33.0 92.2 %copy-start.2 = (bf16[1,7168,256]{2,1,0:T(8,128)(2,1)S(1)}, bf16[1,7168,256]{2,1,0:T(8,128)(2,1)}, u32[]{:S(2)}) copy-start(bf16[1,7168,256]{2,1,0:T(8,128)(2,1)} %param.11) | copy-start | bytes 11010052
  125.2 2.1 copy-start.4
  127.3 2.1 copy-start
  132.5 50.0 %all-to-all-start.2 = ((bf16[32,8,7168]{2,1,0:T(8,128)(2,1)}), bf16[32,8,7168]{2,1,0:T(8,128)(2,1)}, u32[]{:S(2)}, u32[]{:S(2)}) async-start(bf16[32,8,7168]{2,1,0:T(8,128)(2,1)} %fusion.1), calls=%async_computation.2 | async-start | bytes 7340032 | tf_op jit(solution)/shard_map/all_to_all | solution.py:22
  212.5 58.5 %copy-start.1 = (bf16[1,256,7168]{2,1,0:T(8,128)(2,1)S(1)}, bf16[1,256,7168]{2,1,0:T(8,128)(2,1)}, u32[]{:S(2)}) copy-start(bf16[1,256,7168]{2,1,0:T(8,128)(2,1)} %param.13) | copy-start | bytes 11010052
  270.9 2.0 copy-start.3
  273.0 2.0 copy-start.5
  325.0 19.3 %copy-start.6 = (bf16[1,2,7168]{2,1,0:T(2,128)(2,1)S(1)}, bf16[1,2,7168]{2,1,0:T(2,128)(2,1)}, u32[]{:S(2)}) copy-start(bf16[1,2,7168]{2,1,0:T(2,128)(2,1)} %param.8) | copy-start | bytes 86020

commit v7 on v6

--- a/solution.py
+++ b/solution.py
@@ -173,7 +173,7 @@
             jnp.where(lane == 2, jnp.sum(probe_f * probe_f), 0.0),
         ),
     ).astype(F32)
-    sums = total_sum(total_sum(lax.optimization_barrier(sums), "dp"), "expert")
+    sums = total_sum(lax.optimization_barrier(sums), ("dp", "expert"))
     probe_result, result_sq, probe_sq = sums[0, 0], sums[0, 1], sums[0, 2]
     total_cells = lax.axis_size("dp") * lax.axis_size("expert") * tok_dev * model_width
     next_tangent = (result * lax.rsqrt(result_sq / total_cells + 1e-06)).astype(BF16)

time: 375 us -> 372 us (level)
    all_to_all x2 -> x1, blocking collectives: 22.4 us -> 19.7 us  [gather_rows(): return lax.all_to_all(copies, axis, split_axis=0, concat_axis=0, tiled=True)]
where the time goes in v7:
time: 372 us; the launch traced here: 371 us
  blocking collectives  263 us (71%)
  waiting for transfers between devices  61.5 us (17%)
  matrix products  17.3 us (5%)
  starting transfers between devices  13.8 us (4%)
  other arithmetic  6.12 us (2%)
  local copies, waits for them, and re-layouts  5.3 us (1%)
  between operations  4.13 us (1%)
    all_to_all x3, blocking collectives, exchange(): lax.all_to_all(value, 'expert', split_axis=0, concat_axis=0, tiled=True)  199 us
    all_to_all x1, waiting for transfers between devices, exchange(): lax.all_to_all(value, 'expert', split_axis=0, concat_axis=0, tiled=True)  44.9 us
    psum x1, blocking collectives, body(): product_bf = lax.psum(product_part, 'dp').astype(BF16)  26.1 us
    all_to_all x1, blocking collectives, gather_rows(): return lax.all_to_all(copies, axis, split_axis=0, concat_axis=0, tiled=True)  19.7 us
    all_to_all x1, blocking collectives, scatter_sum_rows(): got = lax.all_to_all(value, axis, split_axis=0, concat_axis=0, tiled=True)  18 us
    all_to_all x1, waiting for transfers between devices, gather_rows(): return lax.all_to_all(copies, axis, split_axis=0, concat_axis=0, tiled=True)  16.6 us
    all_to_all x1, starting transfers between devices, gather_rows(): return lax.all_to_all(copies, axis, split_axis=0, concat_axis=0, tiled=True)  9 us
  transfers between devices with their start and end apart: 2, of which 2 were waited for; matrix products, arithmetic and copies ran while one was open for 0% of the time, Pallas kernels for 0%

profile of v7, /device:TPU:1, one launch (start us, length us, event | category | flops | bytes accessed | tf_op | source)
XLA Modules:
  0.0 371.4 jit_solution(2302911760230552139)
XLA Ops:
  2.0 0.9 concatenate.9
  2.9 1.0 broadcast_in_dim.47
  3.9 9.0 %all-to-all-start = ((bf16[8,2,14464]{2,1,0:T(2,128)(2,1)}), bf16[8,2,14464]{2,1,0:T(2,128)(2,1)S(1)}, u32[]{:S(2)}, u32[]{:S(2)}) async-start(bf16[8,2,14464]{2,1,0:T(2,128)(2,1)} %broadcast_in_dim.47), calls=%async_computation | async-start | bytes 925696 | tf_op jit(solution)/shard_map/all_to_all | solution.py:34
  12.9 16.6 %all-to-all-done = bf16[8,2,14464]{2,1,0:T(2,128)(2,1)S(1)} async-done(((bf16[8,2,14464]{2,1,0:T(2,128)(2,1)}), bf16[8,2,14464]{2,1,0:T(2,128)(2,1)S(1)}, u32[]{:S(2)}, u32[]{:S(2)}) %all-to-all-start) | async-done | bytes 462880 | tf_op jit(solution)/shard_map/all_to_all | solution.py:34
  31.0 2.0 convolution_convert_fusion
  33.1 92.2 %all_to_all.44 = bf16[32,16,7168]{2,1,0:T(8,128)(2,1)S(1)} all-to-all(bf16[32,16,7168]{2,1,0:T(8,128)(2,1)S(1)} %bitcast.124), channel_id=1, replica_groups=mesh['dp'=8,'expert'=32] {'expert'}, dimensions={0} | all-to-all | bytes 14680064 | tf_op jit(solution)/shard_map/all_to_all | solution.py:22
  125.2 2.1 fusion.6
  127.3 2.1 fusion.4
  129.4 3.1 fusion.1
  132.5 4.8 %all-to-all-start.2 = ((bf16[32,8,7168]{2,1,0:T(8,128)(2,1)}), bf16[32,8,7168]{2,1,0:T(8,128)(2,1)}, u32[]{:S(2)}, u32[]{:S(2)}) async-start(bf16[32,8,7168]{2,1,0:T(8,128)(2,1)} %fusion.1), calls=%async_computation.2 | async-start | bytes 7340032 | tf_op jit(solution)/shard_map/all_to_all | solution.py:22
  137.5 44.9 %all-to-all-done.2 = bf16[32,8,7168]{2,1,0:T(8,128)(2,1)} async-done(((bf16[32,8,7168]{2,1,0:T(8,128)(2,1)}), bf16[32,8,7168]{2,1,0:T(8,128)(2,1)}, u32[]{:S(2)}, u32[]{:S(2)}) %all-to-all-start.2) | async-done | bytes 3670048 | tf_op jit(solution)/shard_map/all_to_all | solution.py:22
  182.4 2.8 fusion.14
  185.3 26.1 %all-reduce.1 = bf16[16,7168]{1,0:T(8,128)(2,1)S(1)} all-reduce(f32[16,7168]{1,0:T(8,128)S(1)} %slice_add_fusion.1), channel_id=1, replica_groups=mesh['dp'=8,'expert'=32] {'dp'}, use_global_device_ids=true, to_apply=%region_4.5 | all-reduce | flops 114688 | bytes 688128 | tf_op jit(solution)/shard_map/psum | solution.py:149
  211.3 1.1 fusion.2
  212.5 58.5 %all_to_all.45 = bf16[32,8,7168]{2,1,0:T(8,128)(2,1)S(1)} all-to-all(bf16[32,8,7168]{2,1,0:T(8,128)(2,1)S(1)} %fusion.2), channel_id=1, replica_groups=mesh['dp'=8,'expert'=32] {'expert'}, dimensions={0} | all-to-all | bytes 7340032 | tf_op jit(solution)/shard_map/all_to_all | solution.py:22
  271.0 1.1 fusion.12
  272.1 0.9 copy-done.3
  273.0 1.2 fusion.19
  274.2 0.8 copy-done.5
  275.0 1.2 fusion.3
  276.2 48.8 %all_to_all.46 = bf16[32,8,7168]{2,1,0:T(8,128)(2,1)S(1)} all-to-all(bf16[32,8,7168]{2,1,0:T(8,128)(2,1)S(1)} %fusion.3), channel_id=1, replica_groups=mesh['dp'=8,'expert'=32] {'expert'}, dimensions={0} | all-to-all | bytes 7340032 | tf_op jit(solution)/shard_map/all_to_all | solution.py:22
  326.1 18.0 %all_to_all.47 = f32[8,2,7168]{2,1,0:T(2,128)S(1)} all-to-all(f32[8,2,7168]{2,1,0:T(2,128)S(1)} %all_to_all.34), channel_id=1, replica_groups=mesh['dp'=8,'expert'=32] {'dp'}, dimensions={0} | all-to-all | bytes 917504 | tf_op jit(solution)/shard_map/all_to_all | solution.py:39
  345.1 2.0 compare_select_fusion.2
  347.1 19.7 %all_to_all.48 = f32[256,1,128]{2,1,0:T(1,128)S(1)} all-to-all(f32[256,1,128]{2,1,0:T(1,128)S(1)} %reshape.175), channel_id=1, replica_groups=mesh['dp'=8,'expert'=32] {'dp','expert'}, dimensions={0} | all-to-all | bytes 262144 | tf_op jit(solution)/shard_map/all_to_all | solution.py:34
  (43 shorter events, 6.5 us)
Async XLA Ops:
  3.9 25.6 %all-to-all-start = ((bf16[8,2,14464]{2,1,0:T(2,128)(2,1)}), bf16[8,2,14464]{2,1,0:T(2,128)(2,1)S(1)}, u32[]{:S(2)}, u32[]{:S(2)}) async-start(bf16[8,2,14464]{2,1,0:T(2,128)(2,1)} %broadcast_in_dim.47), calls=%async_computation | async-start | bytes 925696 | tf_op jit(solution)/shard_map/all_to_all | solution.py:34
  33.0 92.2 %copy-start.2 = (bf16[1,7168,256]{2,1,0:T(8,128)(2,1)S(1)}, bf16[1,7168,256]{2,1,0:T(8,128)(2,1)}, u32[]{:S(2)}) copy-start(bf16[1,7168,256]{2,1,0:T(8,128)(2,1)} %param.11) | copy-start | bytes 11010052
  125.2 2.1 copy-start.4
  127.3 2.1 copy-start
  132.5 50.0 %all-to-all-start.2 = ((bf16[32,8,7168]{2,1,0:T(8,128)(2,1)}), bf16[32,8,7168]{2,1,0:T(8,128)(2,1)}, u32[]{:S(2)}, u32[]{:S(2)}) async-start(bf16[32,8,7168]{2,1,0:T(8,128)(2,1)} %fusion.1), calls=%async_computation.2 | async-start | bytes 7340032 | tf_op jit(solution)/shard_map/all_to_all | solution.py:22
  212.5 58.5 %copy-start.1 = (bf16[1,256,7168]{2,1,0:T(8,128)(2,1)S(1)}, bf16[1,256,7168]{2,1,0:T(8,128)(2,1)}, u32[]{:S(2)}) copy-start(bf16[1,256,7168]{2,1,0:T(8,128)(2,1)} %param.13) | copy-start | bytes 11010052
  270.9 2.0 copy-start.3
  273.0 2.0 copy-start.5
  325.0 19.3 %copy-start.6 = (bf16[1,2,7168]{2,1,0:T(2,128)(2,1)S(1)}, bf16[1,2,7168]{2,1,0:T(2,128)(2,1)}, u32[]{:S(2)}) copy-start(bf16[1,2,7168]{2,1,0:T(2,128)(2,1)} %param.8) | copy-start | bytes 86020

commit v8 on v7

--- a/solution.py
+++ b/solution.py
@@ -36,8 +36,10 @@
 
 def scatter_sum_rows(value, axis):
     size = lax.axis_size(axis)
-    got = lax.all_to_all(value, axis, split_axis=0, concat_axis=0, tiled=True)
-    return jnp.sum(got.reshape(size, value.shape[0] // size, *value.shape[1:]), axis=0)
+    got = lax.all_to_all(value.astype(BF16), axis, split_axis=0, concat_axis=0, tiled=True)
+    return jnp.sum(
+        got.astype(F32).reshape(size, value.shape[0] // size, *value.shape[1:]), axis=0
+    )
 
 
 def total_sum(value, axis):

time: 372 us -> 367 us (0.987)
  blocking collectives: 263 us -> 258 us
    all_to_all x1, blocking collectives: 18 us -> 13 us  [scatter_sum_rows(): lax.all_to_all(value.astype(BF16), axis, split_axis=0, concat_axis=0, til...]
where the time goes in v8:
time: 367 us; the launch traced here: 366 us
  blocking collectives  258 us (70%)
  waiting for transfers between devices  61.5 us (17%)
  matrix products  17.3 us (5%)
  starting transfers between devices  13.8 us (4%)
  other arithmetic  6.14 us (2%)
  local copies, waits for them, and re-layouts  5.12 us (1%)
  between operations  4.13 us (1%)
    all_to_all x3, blocking collectives, exchange(): lax.all_to_all(value, 'expert', split_axis=0, concat_axis=0, tiled=True)  199 us
    all_to_all x1, waiting for transfers between devices, exchange(): lax.all_to_all(value, 'expert', split_axis=0, concat_axis=0, tiled=True)  44.9 us
    psum x1, blocking collectives, body(): product_bf = lax.psum(product_part, 'dp').astype(BF16)  26.1 us
    all_to_all x1, blocking collectives, gather_rows(): return lax.all_to_all(copies, axis, split_axis=0, concat_axis=0, tiled=True)  19.8 us
    all_to_all x1, waiting for transfers between devices, gather_rows(): return lax.all_to_all(copies, axis, split_axis=0, concat_axis=0, tiled=True)  16.6 us
    all_to_all x1, blocking collectives, scatter_sum_rows(): lax.all_to_all(value.astype(BF16), axis, split_axis=0, concat_axis=0, til...  13 us
    all_to_all x1, starting transfers between devices, gather_rows(): return lax.all_to_all(copies, axis, split_axis=0, concat_axis=0, tiled=True)  9 us
  transfers between devices with their start and end apart: 2, of which 2 were waited for; matrix products, arithmetic and copies ran while one was open for 0% of the time, Pallas kernels for 0%

profile of v8, /device:TPU:1, one launch (start us, length us, event | category | flops | bytes accessed | tf_op | source)
XLA Modules:
  0.0 366.3 jit_solution(7943812327923618978)
XLA Ops:
  2.0 0.9 concatenate.9
  2.9 1.0 broadcast_in_dim.47
  3.9 9.0 %all-to-all-start = ((bf16[8,2,14464]{2,1,0:T(2,128)(2,1)}), bf16[8,2,14464]{2,1,0:T(2,128)(2,1)S(1)}, u32[]{:S(2)}, u32[]{:S(2)}) async-start(bf16[8,2,14464]{2,1,0:T(2,128)(2,1)} %broadcast_in_dim.47), calls=%async_computation | async-start | bytes 925696 | tf_op jit(solution)/shard_map/all_to_all | solution.py:34
  12.9 16.6 %all-to-all-done = bf16[8,2,14464]{2,1,0:T(2,128)(2,1)S(1)} async-done(((bf16[8,2,14464]{2,1,0:T(2,128)(2,1)}), bf16[8,2,14464]{2,1,0:T(2,128)(2,1)S(1)}, u32[]{:S(2)}, u32[]{:S(2)}) %all-to-all-start) | async-done | bytes 462880 | tf_op jit(solution)/shard_map/all_to_all | solution.py:34
  31.0 2.0 convolution_convert_fusion
  33.1 92.2 %all_to_all.44 = bf16[32,16,7168]{2,1,0:T(8,128)(2,1)S(1)} all-to-all(bf16[32,16,7168]{2,1,0:T(8,128)(2,1)S(1)} %bitcast.124), channel_id=1, replica_groups=mesh['dp'=8,'expert'=32] {'expert'}, dimensions={0} | all-to-all | bytes 14680064 | tf_op jit(solution)/shard_map/all_to_all | solution.py:22
  125.2 2.1 fusion.6
  127.3 2.1 fusion.4
  129.4 3.1 fusion.1
  132.5 4.8 %all-to-all-start.2 = ((bf16[32,8,7168]{2,1,0:T(8,128)(2,1)}), bf16[32,8,7168]{2,1,0:T(8,128)(2,1)}, u32[]{:S(2)}, u32[]{:S(2)}) async-start(bf16[32,8,7168]{2,1,0:T(8,128)(2,1)} %fusion.1), calls=%async_computation.2 | async-start | bytes 7340032 | tf_op jit(solution)/shard_map/all_to_all | solution.py:22
  137.5 44.9 %all-to-all-done.2 = bf16[32,8,7168]{2,1,0:T(8,128)(2,1)} async-done(((bf16[32,8,7168]{2,1,0:T(8,128)(2,1)}), bf16[32,8,7168]{2,1,0:T(8,128)(2,1)}, u32[]{:S(2)}, u32[]{:S(2)}) %all-to-all-start.2) | async-done | bytes 3670048 | tf_op jit(solution)/shard_map/all_to_all | solution.py:22
  182.4 2.8 fusion.14
  185.3 26.1 %all-reduce.1 = bf16[16,7168]{1,0:T(8,128)(2,1)S(1)} all-reduce(f32[16,7168]{1,0:T(8,128)S(1)} %slice_add_fusion.1), channel_id=1, replica_groups=mesh['dp'=8,'expert'=32] {'dp'}, use_global_device_ids=true, to_apply=%region_4.5 | all-reduce | flops 114688 | bytes 688128 | tf_op jit(solution)/shard_map/psum | solution.py:151
  211.3 1.1 fusion.2
  212.5 58.5 %all_to_all.45 = bf16[32,8,7168]{2,1,0:T(8,128)(2,1)S(1)} all-to-all(bf16[32,8,7168]{2,1,0:T(8,128)(2,1)S(1)} %fusion.2), channel_id=1, replica_groups=mesh['dp'=8,'expert'=32] {'expert'}, dimensions={0} | all-to-all | bytes 7340032 | tf_op jit(solution)/shard_map/all_to_all | solution.py:22
  271.0 1.1 fusion.12
  272.1 0.9 copy-done.3
  273.0 1.2 fusion.19
  274.2 0.8 copy-done.5
  275.0 1.2 fusion.3
  276.2 48.8 %all_to_all.46 = bf16[32,8,7168]{2,1,0:T(8,128)(2,1)S(1)} all-to-all(bf16[32,8,7168]{2,1,0:T(8,128)(2,1)S(1)} %fusion.3), channel_id=1, replica_groups=mesh['dp'=8,'expert'=32] {'expert'}, dimensions={0} | all-to-all | bytes 7340032 | tf_op jit(solution)/shard_map/all_to_all | solution.py:22
  325.9 13.0 %all_to_all.47 = bf16[8,2,7168]{2,1,0:T(2,128)(2,1)S(1)} all-to-all(bf16[8,2,7168]{2,1,0:T(2,128)(2,1)S(1)} %all_to_all.34), channel_id=1, replica_groups=mesh['dp'=8,'expert'=32] {'dp'}, dimensions={0} | all-to-all | bytes 458752 | tf_op jit(solution)/shard_map/all_to_all | solution.py:39
  339.8 2.0 compare_select_fusion.2
  341.9 19.8 %all_to_all.48 = f32[256,1,128]{2,1,0:T(1,128)S(1)} all-to-all(f32[256,1,128]{2,1,0:T(1,128)S(1)} %reshape.174), channel_id=1, replica_groups=mesh['dp'=8,'expert'=32] {'dp','expert'}, dimensions={0} | all-to-all | bytes 262144 | tf_op jit(solution)/shard_map/all_to_all | solution.py:34
  (43 shorter events, 6.4 us)
Async XLA Ops:
  3.9 25.6 %all-to-all-start = ((bf16[8,2,14464]{2,1,0:T(2,128)(2,1)}), bf16[8,2,14464]{2,1,0:T(2,128)(2,1)S(1)}, u32[]{:S(2)}, u32[]{:S(2)}) async-start(bf16[8,2,14464]{2,1,0:T(2,128)(2,1)} %broadcast_in_dim.47), calls=%async_computation | async-start | bytes 925696 | tf_op jit(solution)/shard_map/all_to_all | solution.py:34
  33.0 92.2 %copy-start.2 = (bf16[1,7168,256]{2,1,0:T(8,128)(2,1)S(1)}, bf16[1,7168,256]{2,1,0:T(8,128)(2,1)}, u32[]{:S(2)}) copy-start(bf16[1,7168,256]{2,1,0:T(8,128)(2,1)} %param.11) | copy-start | bytes 11010052
  125.2 2.1 copy-start.4
  127.3 2.1 copy-start
  132.5 50.0 %all-to-all-start.2 = ((bf16[32,8,7168]{2,1,0:T(8,128)(2,1)}), bf16[32,8,7168]{2,1,0:T(8,128)(2,1)}, u32[]{:S(2)}, u32[]{:S(2)}) async-start(bf16[32,8,7168]{2,1,0:T(8,128)(2,1)} %fusion.1), calls=%async_computation.2 | async-start | bytes 7340032 | tf_op jit(solution)/shard_map/all_to_all | solution.py:22
  212.5 58.5 %copy-start.1 = (bf16[1,256,7168]{2,1,0:T(8,128)(2,1)S(1)}, bf16[1,256,7168]{2,1,0:T(8,128)(2,1)}, u32[]{:S(2)}) copy-start(bf16[1,256,7168]{2,1,0:T(8,128)(2,1)} %param.13) | copy-start | bytes 11010052
  270.9 2.0 copy-start.3
  273.0 2.0 copy-start.5
  325.0 14.0 %copy-start.6 = (bf16[1,2,7168]{2,1,0:T(2,128)(2,1)S(1)}, bf16[1,2,7168]{2,1,0:T(2,128)(2,1)}, u32[]{:S(2)}) copy-start(bf16[1,2,7168]{2,1,0:T(2,128)(2,1)} %param.8) | copy-start | bytes 86020

commit v9 on v8

--- a/solution.py
+++ b/solution.py
@@ -148,7 +148,7 @@
     gate_coef = silu_slope * up_pre
     up_coef = silu_value
     product_part = combine(combine_two, returned.reshape(slot_total, -1))
-    product_bf = lax.psum(product_part, "dp").astype(BF16)
+    product_bf = gather_rows(scatter_sum_rows(product_part, "dp").astype(BF16), "dp")
     send_prod = (
         jnp.dot(route_map, product_bf, preferred_element_type=F32)
         .astype(BF16)

time: 367 us -> 361 us (0.984)
  blocking collectives: 258 us -> 252 us
    psum x1 -> x0, blocking collectives: 26.1 us -> none  [body(): product_bf = lax.psum(product_part, 'dp').astype(BF16)]
    all_to_all x1 -> x2, blocking collectives: 13 us -> 25.3 us  [scatter_sum_rows(): lax.all_to_all(value.astype(BF16), axis, split_axis=0, concat_axis=0, til...]
    all_to_all x1 -> x2, blocking collectives: 19.8 us -> 30 us  [gather_rows(): return lax.all_to_all(copies, axis, split_axis=0, concat_axis=0, tiled=True)]
where the time goes in v9:
time: 361 us
  blocking collectives  252 us (70%)
  waiting for transfers between devices  61.5 us (17%)
  matrix products  17.4 us (5%)
  starting transfers between devices  13.8 us (4%)
  other arithmetic  6.34 us (2%)
  local copies, waits for them, and re-layouts  5.41 us (1%)
  between operations  4.14 us (1%)
    all_to_all x3, blocking collectives, exchange(): lax.all_to_all(value, 'expert', split_axis=0, concat_axis=0, tiled=True)  197 us
    all_to_all x1, waiting for transfers between devices, exchange(): lax.all_to_all(value, 'expert', split_axis=0, concat_axis=0, tiled=True)  44.9 us
    all_to_all x2, blocking collectives, gather_rows(): return lax.all_to_all(copies, axis, split_axis=0, concat_axis=0, tiled=True)  30 us
    all_to_all x2, blocking collectives, scatter_sum_rows(): lax.all_to_all(value.astype(BF16), axis, split_axis=0, concat_axis=0, til...  25.3 us
    all_to_all x1, waiting for transfers between devices, gather_rows(): return lax.all_to_all(copies, axis, split_axis=0, concat_axis=0, tiled=True)  16.6 us
    all_to_all x1, starting transfers between devices, gather_rows(): return lax.all_to_all(copies, axis, split_axis=0, concat_axis=0, tiled=True)  9 us
  transfers between devices with their start and end apart: 2, of which 2 were waited for; matrix products, arithmetic and copies ran while one was open for 0% of the time, Pallas kernels for 0%

profile of v9, /device:TPU:1, one launch (start us, length us, event | category | flops | bytes accessed | tf_op | source)
XLA Modules:
  0.0 360.6 jit_solution(14048184357937838577)
XLA Ops:
  2.0 0.9 concatenate.9
  2.9 1.0 broadcast_in_dim.53
  3.9 9.0 %all-to-all-start = ((bf16[8,2,14464]{2,1,0:T(2,128)(2,1)}), bf16[8,2,14464]{2,1,0:T(2,128)(2,1)S(1)}, u32[]{:S(2)}, u32[]{:S(2)}) async-start(bf16[8,2,14464]{2,1,0:T(2,128)(2,1)} %broadcast_in_dim.53), calls=%async_computation | async-start | bytes 925696 | tf_op jit(solution)/shard_map/all_to_all | solution.py:34
  12.9 16.6 %all-to-all-done = bf16[8,2,14464]{2,1,0:T(2,128)(2,1)S(1)} async-done(((bf16[8,2,14464]{2,1,0:T(2,128)(2,1)}), bf16[8,2,14464]{2,1,0:T(2,128)(2,1)S(1)}, u32[]{:S(2)}, u32[]{:S(2)}) %all-to-all-start) | async-done | bytes 462880 | tf_op jit(solution)/shard_map/all_to_all | solution.py:34
  31.0 2.0 convolution_convert_fusion
  33.1 92.2 %all_to_all.62 = bf16[32,16,7168]{2,1,0:T(8,128)(2,1)S(1)} all-to-all(bf16[32,16,7168]{2,1,0:T(8,128)(2,1)S(1)} %bitcast.124), channel_id=1, replica_groups=mesh['dp'=8,'expert'=32] {'expert'}, dimensions={0} | all-to-all | bytes 14680064 | tf_op jit(solution)/shard_map/all_to_all | solution.py:22
  125.2 2.1 fusion.6
  127.3 2.1 fusion.4
  129.4 3.1 fusion.1
  132.5 4.8 %all-to-all-start.2 = ((bf16[32,8,7168]{2,1,0:T(8,128)(2,1)}), bf16[32,8,7168]{2,1,0:T(8,128)(2,1)}, u32[]{:S(2)}, u32[]{:S(2)}) async-start(bf16[32,8,7168]{2,1,0:T(8,128)(2,1)} %fusion.1), calls=%async_computation.2 | async-start | bytes 7340032 | tf_op jit(solution)/shard_map/all_to_all | solution.py:22
  137.5 44.9 %all-to-all-done.2 = bf16[32,8,7168]{2,1,0:T(8,128)(2,1)} async-done(((bf16[32,8,7168]{2,1,0:T(8,128)(2,1)}), bf16[32,8,7168]{2,1,0:T(8,128)(2,1)}, u32[]{:S(2)}, u32[]{:S(2)}) %all-to-all-start.2) | async-done | bytes 3670048 | tf_op jit(solution)/shard_map/all_to_all | solution.py:22
  182.4 2.8 fusion.14
  185.3 11.4 %all_to_all.63 = bf16[8,2,7168]{2,1,0:T(2,128)(2,1)S(1)} all-to-all(bf16[8,2,7168]{2,1,0:T(2,128)(2,1)S(1)} %all_to_all.44), channel_id=1, replica_groups=mesh['dp'=8,'expert'=32] {'dp'}, dimensions={0} | all-to-all | bytes 458752 | tf_op jit(solution)/shard_map/all_to_all | solution.py:39
  197.1 11.5 %all_to_all.64 = bf16[8,2,7168]{2,1,0:T(2,128)(2,1)S(1)} all-to-all(bf16[8,2,7168]{2,1,0:T(2,128)(2,1)S(1)} %broadcast_in_dim.56), channel_id=1, replica_groups=mesh['dp'=8,'expert'=32] {'dp'}, dimensions={0} | all-to-all | bytes 458752 | tf_op jit(solution)/shard_map/all_to_all | solution.py:34
  208.7 1.1 fusion.2
  209.8 55.9 %all_to_all.65 = bf16[32,8,7168]{2,1,0:T(8,128)(2,1)S(1)} all-to-all(bf16[32,8,7168]{2,1,0:T(8,128)(2,1)S(1)} %fusion.2), channel_id=1, replica_groups=mesh['dp'=8,'expert'=32] {'expert'}, dimensions={0} | all-to-all | bytes 7340032 | tf_op jit(solution)/shard_map/all_to_all | solution.py:22
  265.7 1.1 fusion.12
  266.9 0.9 copy-done.3
  267.8 1.2 fusion.19
  269.8 1.2 fusion.3
  271.0 48.8 %all_to_all.66 = bf16[32,8,7168]{2,1,0:T(8,128)(2,1)S(1)} all-to-all(bf16[32,8,7168]{2,1,0:T(8,128)(2,1)S(1)} %fusion.3), channel_id=1, replica_groups=mesh['dp'=8,'expert'=32] {'expert'}, dimensions={0} | all-to-all | bytes 7340032 | tf_op jit(solution)/shard_map/all_to_all | solution.py:22
  320.6 13.9 %all_to_all.67 = bf16[8,2,7168]{2,1,0:T(2,128)(2,1)S(1)} all-to-all(bf16[8,2,7168]{2,1,0:T(2,128)(2,1)S(1)} %all_to_all.50), channel_id=1, replica_groups=mesh['dp'=8,'expert'=32] {'dp'}, dimensions={0} | all-to-all | bytes 458752 | tf_op jit(solution)/shard_map/all_to_all | solution.py:39
  335.5 2.0 compare_select_fusion.2
  337.6 18.5 %all_to_all.68 = f32[256,1,128]{2,1,0:T(1,128)S(1)} all-to-all(f32[256,1,128]{2,1,0:T(1,128)S(1)} %reshape.184), channel_id=1, replica_groups=mesh['dp'=8,'expert'=32] {'dp','expert'}, dimensions={0} | all-to-all | bytes 262144 | tf_op jit(solution)/shard_map/all_to_all | solution.py:34
  (48 shorter events, 7.7 us)
Async XLA Ops:
  3.9 25.6 %all-to-all-start = ((bf16[8,2,14464]{2,1,0:T(2,128)(2,1)}), bf16[8,2,14464]{2,1,0:T(2,128)(2,1)S(1)}, u32[]{:S(2)}, u32[]{:S(2)}) async-start(bf16[8,2,14464]{2,1,0:T(2,128)(2,1)} %broadcast_in_dim.53), calls=%async_computation | async-start | bytes 925696 | tf_op jit(solution)/shard_map/all_to_all | solution.py:34
  33.0 92.2 %copy-start.2 = (bf16[1,7168,256]{2,1,0:T(8,128)(2,1)S(1)}, bf16[1,7168,256]{2,1,0:T(8,128)(2,1)}, u32[]{:S(2)}) copy-start(bf16[1,7168,256]{2,1,0:T(8,128)(2,1)} %param.11) | copy-start | bytes 11010052
  125.2 2.1 copy-start.4
  127.3 2.1 copy-start
  132.5 50.0 %all-to-all-start.2 = ((bf16[32,8,7168]{2,1,0:T(8,128)(2,1)}), bf16[32,8,7168]{2,1,0:T(8,128)(2,1)}, u32[]{:S(2)}, u32[]{:S(2)}) async-start(bf16[32,8,7168]{2,1,0:T(8,128)(2,1)} %fusion.1), calls=%async_computation.2 | async-start | bytes 7340032 | tf_op jit(solution)/shard_map/all_to_all | solution.py:22
  209.8 55.9 %copy-start.1 = (bf16[1,256,7168]{2,1,0:T(8,128)(2,1)S(1)}, bf16[1,256,7168]{2,1,0:T(8,128)(2,1)}, u32[]{:S(2)}) copy-start(bf16[1,256,7168]{2,1,0:T(8,128)(2,1)} %param.13) | copy-start | bytes 11010052
  265.7 2.0 copy-start.3
  267.8 2.0 copy-start.5
  319.7 15.0 %copy-start.6 = (bf16[1,2,7168]{2,1,0:T(2,128)(2,1)S(1)}, bf16[1,2,7168]{2,1,0:T(2,128)(2,1)}, u32[]{:S(2)}) copy-start(bf16[1,2,7168]{2,1,0:T(2,128)(2,1)} %param.8) | copy-start | bytes 86020
